TPU v7x, 256 devices: a whole 4x4x8 slice. The times are simulated.
256 devices in a mesh: pipe: 8 (over z_hi, core), tensor: 8 (over z_lo, y), dp: 4 (over x).
Axes of the slice: x: 4, y: 4, z: 8 (z_hi: 4, z_lo: 2; z = z_hi * 2 + z_lo), core: 2. Of those that a mesh axis runs over, the one named last changes fastest.
Arguments:
- queries: bfloat16 [8, 4, 1024, 6144], P('pipe', 'dp', None, 'tensor'), may hold values from -128 to 128
- key_heads: bfloat16 [8, 4, 1024, 6144], P('pipe', 'dp', None, 'tensor'), may hold values from -6 to 6
- value_heads: bfloat16 [8, 4, 1024, 6144], P('pipe', 'dp', None, 'tensor'), may hold values from -6 to 6
- context_grad: bfloat16 [8, 4, 1024, 6144], P('pipe', 'dp', None, 'tensor'), may hold values from -6 to 6
- output_grad: bfloat16 [8, 4, 1024, 6144], P('pipe', 'dp', 'tensor'), may hold values from -6 to 6
- random_blocks: int32 [48, 14, 3], P('tensor'), may hold values from 1 to 14, as said below
Outputs:
- query_grad: bfloat16 [8, 4, 1024, 6144], P('pipe', 'dp', None, 'tensor')
- key_grad: bfloat16 [8, 4, 1024, 6144], P('pipe', 'dp', None, 'tensor')
- value_grad: bfloat16 [8, 4, 1024, 6144], P('pipe', 'dp', None, 'tensor')
- weight_grad: bfloat16 [8, 3072, 6144], P('pipe', 'dp', 'tensor')
Inputs may be any that keep to these rules, and one draw needn't show every extreme that they name: `random_blocks`: in row r (query block r + 1) the 3 entries are distinct, none is 0 or 16 - 1, and none lies within one block of r + 1.
All inputs are finite; a program needn't handle non-finite values.
Results may differ from a plain program's by a relative error of at most 0.029.
Values may be sent and summed in bfloat16 or wider, within the bound.
No kernel may reach another device: no remote copies, remote signals or barrier semaphores. Data moves between devices by JAX's collectives and lax.ppermute only.
A program may use at most 256 MiB of HBM per device.

v0:
```python
import functools
import math

import jax
import jax.numpy as jnp
from jax import lax
from jax.experimental import pallas as pl
from jax.experimental.pallas import tpu as pltpu
from jax.sharding import PartitionSpec as P

BLK = 64
ROWS = 256


def attention_kernel(
    blocks, head_size, rb_ref, q_ref, k_ref, v_ref, g_ref, dq_ref, ctx_ref, dk_ref, dv_ref,
    dk_acc, dv_acc,
):
    head = pl.program_id(0)
    chunk = pl.program_id(1)
    score_scale = 1.0 / math.sqrt(head_size)
    tokens = k_ref.shape[0]
    per_chunk = q_ref.shape[0] // BLK
    mids = blocks - 2

    @pl.when(chunk == 0)
    def _():
        dk_acc[...] = jnp.zeros_like(dk_acc)
        dv_acc[...] = jnp.zeros_like(dv_acc)

    q = q_ref[...]
    k = k_ref[...]
    v = v_ref[...]
    g = g_ref[...]
    scores = lax.dot_general(
        q, k, (((1,), (1,)), ((), ())), preferred_element_type=jnp.float32
    ) * score_scale
    key_block = lax.broadcasted_iota(jnp.int32, (1, tokens), 1) // BLK
    bias_rows = []
    for i in range(per_chunk):
        qb = chunk * per_chunk + i
        row = jnp.clip(qb - 1, 0, mids - 1)
        base = (head * mids + row) * 3
        r1 = rb_ref[base]
        r2 = rb_ref[base + 1]
        r3 = rb_ref[base + 2]
        edge = jnp.logical_or(qb == 0, qb == blocks - 1)
        near = jnp.abs(key_block - qb) <= 1
        allowed = (
            (key_block == 0)
            | (key_block == blocks - 1)
            | near
            | (key_block == r1)
            | (key_block == r2)
            | (key_block == r3)
            | edge
        )
        bias = jnp.where(allowed, 0.0, -1e30).astype(jnp.float32)
        bias_rows.append(jnp.broadcast_to(bias, (BLK, tokens)))
    scores = scores + jnp.concatenate(bias_rows, axis=0)
    row_peak = jnp.max(scores, axis=1, keepdims=True)
    raised = jnp.exp(scores - row_peak)
    prob = raised / jnp.sum(raised, axis=1, keepdims=True)
    prob_b = prob.astype(jnp.bfloat16)
    ctx = jnp.dot(prob_b, v, preferred_element_type=jnp.float32).astype(jnp.bfloat16)
    ctx_ref[...] = ctx
    dprob = lax.dot_general(
        g, v, (((1,), (1,)), ((), ())), preferred_element_type=jnp.float32
    )
    row_dot = jnp.sum(
        g.astype(jnp.float32) * ctx.astype(jnp.float32), axis=1, keepdims=True
    )
    dscore = (prob * (dprob - row_dot)).astype(jnp.bfloat16)
    dq = jnp.dot(dscore, k, preferred_element_type=jnp.float32) * score_scale
    dq_ref[...] = dq.astype(jnp.bfloat16)
    dk_acc[...] += lax.dot_general(
        dscore, q, (((0,), (0,)), ((), ())), preferred_element_type=jnp.float32
    )
    dv_acc[...] += lax.dot_general(
        prob_b, g, (((0,), (0,)), ((), ())), preferred_element_type=jnp.float32
    )

    @pl.when(chunk == pl.num_programs(1) - 1)
    def _():
        dk_ref[...] = (dk_acc[...] * score_scale).astype(jnp.bfloat16)
        dv_ref[...] = dv_acc[...].astype(jnp.bfloat16)


def attention_backward(queries, key_heads, value_heads, context_grad, random_blocks):
    heads_here = random_blocks.shape[0]
    tokens, width_here = queries.shape
    head_size = width_here // heads_here
    blocks = tokens // BLK
    chunks = tokens // ROWS
    rb_flat = random_blocks.reshape(-1)
    row_spec = pl.BlockSpec((ROWS, head_size), lambda h, c, rb: (c, h))
    full_spec = pl.BlockSpec((tokens, head_size), lambda h, c, rb: (0, h))
    out_shape = jax.ShapeDtypeStruct((tokens, width_here), jnp.bfloat16)
    flops = 2 * tokens * tokens * head_size * 6 * heads_here
    call = pl.pallas_call(
        functools.partial(attention_kernel, blocks, head_size),
        out_shape=(out_shape, out_shape, out_shape, out_shape),
        grid_spec=pltpu.PrefetchScalarGridSpec(
            num_scalar_prefetch=1,
            grid=(heads_here, chunks),
            in_specs=[row_spec, full_spec, full_spec, row_spec],
            out_specs=[row_spec, row_spec, full_spec, full_spec],
            scratch_shapes=[
                pltpu.VMEM((tokens, head_size), jnp.float32),
                pltpu.VMEM((tokens, head_size), jnp.float32),
            ],
        ),
        compiler_params=pltpu.CompilerParams(
            dimension_semantics=("arbitrary", "arbitrary"),
            vmem_limit_bytes=48 * 1024 * 1024,
        ),
        cost_estimate=pl.CostEstimate(
            flops=flops,
            transcendentals=tokens * tokens * heads_here,
            bytes_accessed=7 * tokens * width_here * 2,
        ),
    )
    query_grad, context, key_grad, value_grad = call(
        rb_flat, queries, key_heads, value_heads, context_grad
    )
    return query_grad, key_grad, value_grad, context


def shift_over(block, axis, shift):
    count = lax.axis_size(axis)
    return lax.ppermute(block, axis, [(i, (i + shift) % count) for i in range(count)])


def on_device(queries, key_heads, value_heads, context_grad, output_grad, random_blocks):
    dp_count = lax.axis_size("dp")
    dp_pos = lax.axis_index("dp")
    rows_here = output_grad.shape[2]
    width_model = output_grad.shape[3]
    quarter = width_model // (2 * dp_count)
    pieces = output_grad[0, 0].reshape(rows_here, 2, dp_count, quarter).transpose(2, 0, 1, 3)
    received = [None] * dp_count
    received_own = lax.dynamic_index_in_dim(pieces, dp_pos, 0, keepdims=False)
    for shift in range(1, dp_count):
        target = (dp_pos + shift) % dp_count
        outgoing = lax.dynamic_index_in_dim(pieces, target, 0, keepdims=False)
        received[shift] = shift_over(outgoing, "dp", shift)
    received[0] = received_own
    moved_cols = jnp.stack(received)
    columns = lax.all_gather(moved_cols, "tensor", axis=1, tiled=True)

    query_grad, key_grad, value_grad, ctx_rows = attention_backward(
        queries[0, 0], key_heads[0, 0], value_heads[0, 0], context_grad[0, 0], random_blocks
    )
    tokens_all, width_here = ctx_rows.shape
    ctx_parts = [None] * dp_count
    ctx_parts[0] = ctx_rows
    for shift in range(1, dp_count):
        ctx_parts[shift] = shift_over(ctx_rows, "dp", shift)
    contexts = jnp.stack(ctx_parts)

    summed = lax.dot_general(
        columns.reshape(dp_count * tokens_all, 2 * quarter),
        contexts.reshape(dp_count * tokens_all, width_here),
        (((0,), (0,)), ((), ())),
        preferred_element_type=jnp.float32,
    ).reshape(2, quarter, width_here)
    summed_b = summed.astype(jnp.bfloat16)
    pipe_count = lax.axis_size("pipe")
    pipe_pos = lax.axis_index("pipe")
    upper_half = (pipe_pos >= pipe_count // 2).astype(jnp.int32)
    own_half = lax.dynamic_index_in_dim(summed_b, upper_half, 0, keepdims=False)
    outgoing = lax.dynamic_index_in_dim(summed_b, 1 - upper_half, 0, keepdims=False)
    incoming = lax.ppermute(
        outgoing, "pipe", [(i, pipe_count - 1 - i) for i in range(pipe_count)]
    )
    weight_grad = (own_half.astype(jnp.float32) + incoming.astype(jnp.float32)).astype(
        jnp.bfloat16
    )[None]
    shape4 = queries.shape
    return (
        query_grad.reshape(shape4),
        key_grad.reshape(shape4),
        value_grad.reshape(shape4),
        weight_grad,
    )


def solution(mesh):
    in_specs = (
        P("pipe", "dp", None, "tensor"),
        P("pipe", "dp", None, "tensor"),
        P("pipe", "dp", None, "tensor"),
        P("pipe", "dp", None, "tensor"),
        P("pipe", "dp", "tensor", None),
        P("tensor", None, None),
    )
    out_specs = (
        P("pipe", "dp", None, "tensor"),
        P("pipe", "dp", None, "tensor"),
        P("pipe", "dp", None, "tensor"),
        P("pipe", "dp", "tensor"),
    )
    return jax.shard_map(
        on_device, mesh=mesh, in_specs=in_specs, out_specs=out_specs, check_vma=False
    )
```

profile of v0, /device:TPU:1, one launch (start us, length us, event | category | flops | bytes accessed | tf_op | source)
XLA Modules:
  0.0 298.0 jit_solution(9521750946094278952)
XLA Ops:
  7.3 1.9 copy.12
  9.2 0.1 constant_dynamic-slice_fusion.3
  9.3 0.2 copy.14
  9.5 2.1 collective-permute-start
  11.6 0.2 copy.15
  11.8 2.5 collective-permute-start.1
  14.3 0.2 copy.16
  14.5 1.2 collective-permute-start.2
  15.7 0.2 copy.13
  15.9 3.6 %collective-permute-done = bf16[128,2,768]{2,0,1:T(8,128)(2,1)S(1)} collective-permute-done((bf16[128,2,768]{2,0,1:T(8,128)(2,1)S(1)}, bf16[128,2,768]{2,0,1:T(8,128)(2,1)S(1)}, u32[]{:S(2)}, u32[]{:S(2)}) %collective-permute-start) | collective-permute-done | bytes 393248 | tf_op jit(solution)/shard_map/ppermute | solution.py:131
  19.5 11.5 %collective-permute-done.1 = bf16[128,2,768]{2,0,1:T(8,128)(2,1)S(1)} collective-permute-done((bf16[128,2,768]{2,0,1:T(8,128)(2,1)S(1)}, bf16[128,2,768]{2,0,1:T(8,128)(2,1)S(1)}, u32[]{:S(2)}, u32[]{:S(2)}) %collective-permute-start.1) | collective-permute-done | bytes 393248 | tf_op jit(solution)/shard_map/ppermute | solution.py:131
  31.0 1.4 pad_maximum_fusion.1
  32.4 0.1 copy.11
  32.6 0.2 reshape.37.rb_ref
  32.7 1.1 copy-done
  33.8 1.4 copy-done.1
  35.2 37.8 %shard_map.93 = (bf16[1024,768]{1,0:T(8,128)(2,1)}, bf16[1024,768]{1,0:T(8,128)(2,1)S(1)}, bf16[1024,768]{1,0:T(8,128)(2,1)}, bf16[1024,768]{1,0:T(8,128)(2,1)}) custom-call(s32[252]{0:T(256)S(1)} %reshape.37.rb_ref, bf16[1024,768]{1,0:T(8,128)(2,1)S(1)} %bitcast.38, bf16[1024,768]{1,0:T(8,128)(2,1)S(1)} %bitcast.39, bf16[1024,768]{1,0:T(8,128)(2,1)} %bitcast.53, ...), custom_call_target="tpu_custom_call" | custom-call | flops 9663676416 | bytes 11010048 | tf_op jit(solution)/shard_map/pallas_call | solution.py:123
  73.0 1.8 collective-permute-start.3
  74.8 2.4 collective-permute-start.4
  77.2 0.2 collective-permute-start.5
  77.4 32.1 %collective-permute-done.3 = bf16[1024,768]{1,0:T(8,128)(2,1)S(1)} collective-permute-done((bf16[1024,768]{1,0:T(8,128)(2,1)S(1)}, bf16[1024,768]{1,0:T(8,128)(2,1)S(1)}, u32[]{:S(2)}, u32[]{:S(2)}) %collective-permute-start.3) | collective-permute-done | bytes 1572896 | tf_op jit(solution)/shard_map/ppermute | solution.py:131
  109.6 35.5 %collective-permute-done.4 = bf16[1024,768]{1,0:T(8,128)(2,1)} collective-permute-done((bf16[1024,768]{1,0:T(8,128)(2,1)S(1)}, bf16[1024,768]{1,0:T(8,128)(2,1)}, u32[]{:S(2)}, u32[]{:S(2)}) %collective-permute-start.4) | collective-permute-done | bytes 1572896 | tf_op jit(solution)/shard_map/ppermute | solution.py:131
  145.1 5.2 %pad_maximum_fusion = bf16[4,1024,768]{2,1,0:T(8,128)(2,1)} fusion(bf16[1,1024,768]{2,1,0:T(8,128)(2,1)} %bitcast.20, bf16[1,1024,768]{2,1,0:T(8,128)(2,1)} %bitcast.19, bf16[1,1024,768]{2,1,0:T(8,128)(2,1)S(1)} %bitcast.45, bf16[1,1024,768]{2,1,0:T(8,128)(2,1)S(1)} %bitcast.37), kind=kLoop, calls=%fused_computation | loop fusion | flops 9437184 | bytes 12582912 | tf_op jit(solution)/shard_map/stack | solution.py:159
  150.2 19.7 %all-gather.2.cloned.1.call-done = bf16[4,1024,2,768]{3,1,2,0:T(8,128)(2,1)} async-done(((bf16[4,128,2,768]{3,1,2,0:T(8,128)(2,1)}), bf16[4,1024,2,768]{3,1,2,0:T(8,128)(2,1)}) %all-gather.2.cloned.1.call-update) | async-done | bytes 12582928 | tf_op jit(solution)/shard_map/all_gather | solution.py:149
  170.0 23.1 %copy.17 = bf16[4,1024,2,768]{3,2,1,0:T(2,128)(2,1)S(1)} copy(bf16[4,1024,2,768]{3,1,2,0:T(8,128)(2,1)} %all-gather.2.cloned.1.call-done) | data formatting | bytes 25165824 | tf_op jit(solution)/shard_map/all_gather | solution.py:149
  193.1 9.4 %copy.19 = bf16[512,8,2,768]{3,1,2,0:T(8,128)(2,1)} copy(bf16[512,8,2,768]{3,2,1,0:T(2,128)(2,1)S(1)} %bitcast.40) | data formatting | bytes 25165824
  202.5 16.6 %copy.18 = bf16[1536,4096]{1,0:T(8,128)(2,1)} copy(bf16[1536,4096]{0,1:T(8,128)(2,1)} %bitcast.41) | data formatting | bytes 25165824 | tf_op jit(solution)/shard_map/dot_general | solution.py:161
  219.1 14.7 %convolution_convert_fusion = bf16[2,768,768]{2,1,0:T(8,128)(2,1)S(1)} fusion(bf16[2,768,4096]{2,1,0:T(8,128)(2,1)} %bitcast.42, bf16[4096,768,1]{1,0,2:T(8,128)(2,1)} %bitcast.43), kind=kOutput, calls=%fused_computation.3 | convolution fusion | flops 9664856064 | bytes 21233664 | tf_op jit(solution)/shard_map/dot_general | solution.py:161
  233.8 0.1 dynamic-slice_bitcast_fusion
  233.9 3.7 %collective-permute-start.6 = (bf16[768,768]{1,0:T(8,128)(2,1)S(1)}, bf16[768,768]{1,0:T(8,128)(2,1)}, u32[]{:S(2)}, u32[]{:S(2)}) collective-permute-start(bf16[768,768]{1,0:T(8,128)(2,1)S(1)} %dynamic-slice_bitcast_fusion), channel_id=1, source_target_pairs={{0,224},{32,192},{64,160},{96,128},{128,96},{160,64},{192,32},{224... | collective-permute-start | bytes 3538952 | tf_op jit(solution)/shard_map/ppermute | solution.py:173
  237.7 50.9 %collective-permute-done.6 = bf16[768,768]{1,0:T(8,128)(2,1)} collective-permute-done((bf16[768,768]{1,0:T(8,128)(2,1)S(1)}, bf16[768,768]{1,0:T(8,128)(2,1)}, u32[]{:S(2)}, u32[]{:S(2)}) %collective-permute-start.6) | collective-permute-done | bytes 1179680 | tf_op jit(solution)/shard_map/ppermute | solution.py:173
  288.6 2.6 fusion.1
  (8 shorter events, 0.1 us)
Async XLA Ops:
  7.2 162.8 %all-gather.2.cloned.1.call-start = ((), (), s32[]{:S(2)}) async-start(), calls=%async_computation | async-start | bytes 14155776 | tf_op jit(solution)/shard_map/all_gather | solution.py:149
  9.5 10.0 %collective-permute-start = (bf16[128,2,768]{2,0,1:T(8,128)(2,1)S(1)}, bf16[128,2,768]{2,0,1:T(8,128)(2,1)S(1)}, u32[]{:S(2)}, u32[]{:S(2)}) collective-permute-start(bf16[128,2,768]{2,0,1:T(8,128)(2,1)S(1)} %bitcast.50), channel_id=1, source_target_pairs={{0,1},{1,2},{2,3},{3,0},{4,5},{5,6},{6,7},{7,4},{8,9},{9,10},{10,1... | collective-permute-start | bytes 1179656 | tf_op jit(solution)/shard_map/ppermute | solution.py:131
  11.8 19.2 %collective-permute-start.1 = (bf16[128,2,768]{2,0,1:T(8,128)(2,1)S(1)}, bf16[128,2,768]{2,0,1:T(8,128)(2,1)S(1)}, u32[]{:S(2)}, u32[]{:S(2)}) collective-permute-start(bf16[128,2,768]{2,0,1:T(8,128)(2,1)S(1)} %bitcast.51), channel_id=1, source_target_pairs={{0,2},{1,3},{2,0},{3,1},{4,6},{5,7},{6,4},{7,5},{8,10},{9,11},{10,... | collective-permute-start | bytes 1179656 | tf_op jit(solution)/shard_map/ppermute | solution.py:131
  14.5 16.5 %collective-permute-start.2 = (bf16[128,2,768]{2,0,1:T(8,128)(2,1)S(1)}, bf16[128,2,768]{2,0,1:T(8,128)(2,1)S(1)}, u32[]{:S(2)}, u32[]{:S(2)}) collective-permute-start(bf16[128,2,768]{2,0,1:T(8,128)(2,1)S(1)} %bitcast.52), channel_id=1, source_target_pairs={{0,3},{1,0},{2,1},{3,2},{4,7},{5,4},{6,5},{7,6},{8,11},{9,8},{10,9... | collective-permute-start | bytes 1179656 | tf_op jit(solution)/shard_map/ppermute | solution.py:131
  31.0 1.4 copy-start.2
  32.4 1.4 copy-start
  33.8 1.4 copy-start.1
  73.0 36.6 %collective-permute-start.3 = (bf16[1024,768]{1,0:T(8,128)(2,1)S(1)}, bf16[1024,768]{1,0:T(8,128)(2,1)S(1)}, u32[]{:S(2)}, u32[]{:S(2)}) collective-permute-start(bf16[1024,768]{1,0:T(8,128)(2,1)S(1)} %get-tuple-element.11), channel_id=1, source_target_pairs={{0,1},{1,2},{2,3},{3,0},{4,5},{5,6},{6,7},{7,4},{8,9},{9,10},{10,1... | collective-permute-start | bytes 4718600 | tf_op jit(solution)/shard_map/ppermute | solution.py:131
  74.8 70.2 %collective-permute-start.4 = (bf16[1024,768]{1,0:T(8,128)(2,1)S(1)}, bf16[1024,768]{1,0:T(8,128)(2,1)}, u32[]{:S(2)}, u32[]{:S(2)}) collective-permute-start(bf16[1024,768]{1,0:T(8,128)(2,1)S(1)} %get-tuple-element.11), channel_id=1, source_target_pairs={{0,2},{1,3},{2,0},{3,1},{4,6},{5,7},{6,4},{7,5},{8,10},{9,11},{10,... | collective-permute-start | bytes 4718600 | tf_op jit(solution)/shard_map/ppermute | solution.py:131
  77.2 67.8 %collective-permute-start.5 = (bf16[1024,768]{1,0:T(8,128)(2,1)S(1)}, bf16[1024,768]{1,0:T(8,128)(2,1)}, u32[]{:S(2)}, u32[]{:S(2)}) collective-permute-start(bf16[1024,768]{1,0:T(8,128)(2,1)S(1)} %get-tuple-element.11), channel_id=1, source_target_pairs={{0,3},{1,0},{2,1},{3,2},{4,7},{5,4},{6,5},{7,6},{8,11},{9,8},{10,9... | collective-permute-start | bytes 4718600 | tf_op jit(solution)/shard_map/ppermute | solution.py:131
  233.9 54.7 %collective-permute-start.6 = (bf16[768,768]{1,0:T(8,128)(2,1)S(1)}, bf16[768,768]{1,0:T(8,128)(2,1)}, u32[]{:S(2)}, u32[]{:S(2)}) collective-permute-start(bf16[768,768]{1,0:T(8,128)(2,1)S(1)} %dynamic-slice_bitcast_fusion), channel_id=1, source_target_pairs={{0,224},{32,192},{64,160},{96,128},{128,96},{160,64},{192,32},{224... | collective-permute-start | bytes 3538952 | tf_op jit(solution)/shard_map/ppermute | solution.py:173
Sparse Core Ops, SparseCore 0:
  32.5 137.3 all-gather.1
where the time goes:
time: 299 us; the launch traced here: 298 us
  waiting for transfers between devices  153 us (51%)
  local copies, waits for them, and re-layouts  54.8 us (18%)
  Pallas kernels  37.8 us (13%)
  matrix products  14.7 us (5%)
  between operations  14.2 us (5%)
  starting transfers between devices  14.1 us (5%)
  other arithmetic  9.12 us (3%)
    ppermute x6, waiting for transfers between devices, shift_over(): lax.ppermute(block, axis, [(i, (i + shift) % count) for i in range(count)])  82.7 us
    ppermute x1, waiting for transfers between devices, on_device(): lax.ppermute(outgoing, 'pipe', [(i, pipe_count - 1 - i) for i in range(pi...  50.9 us
    pallas_call x1, Pallas kernels, attention_backward(): call(rb_flat, queries, key_heads, value_heads, context_grad)  37.8 us
    all_gather x1, local copies, waits for them, and re-layouts, on_device(): columns = lax.all_gather(moved_cols, 'tensor', axis=1, tiled=True)  23.1 us
    all_gather x1, waiting for transfers between devices, on_device(): columns = lax.all_gather(moved_cols, 'tensor', axis=1, tiled=True)  19.7 us
    dot_general x1, local copies, waits for them, and re-layouts, on_device(): lax.dot_general(columns.reshape(dp_count * tokens_all, 2 * quarter), cont...  16.6 us
    dot_general x1, matrix products, on_device(): lax.dot_general(columns.reshape(dp_count * tokens_all, 2 * quarter), cont...  14.7 us
    unnamed x9, local copies, waits for them, and re-layouts  13.9 us
  transfers between devices with their start and end apart: 8, of which 6 were waited for; matrix products, arithmetic and copies ran while one was open for 2% of the time, Pallas kernels for 13%

commit v1 on v0

--- a/solution.py
+++ b/solution.py
@@ -131,49 +131,102 @@
     return lax.ppermute(block, axis, [(i, (i + shift) % count) for i in range(count)])
 
 
+def wgrad_kernel(cols_ref, own_ref, left_ref, far_lo_ref, far_hi_ref, right_ref, out_ref, acc):
+    slot = pl.program_id(0)
+    half = far_lo_ref.shape[0]
+
+    def term(cols, ctx):
+        return lax.dot_general(
+            cols, ctx, (((0,), (0,)), ((), ())), preferred_element_type=jnp.float32
+        )
+
+    @pl.when(slot == 0)
+    def _():
+        acc[...] = term(cols_ref[...], own_ref[...])
+
+    @pl.when(slot == 1)
+    def _():
+        acc[...] += term(cols_ref[...], left_ref[...])
+
+    @pl.when(slot == 2)
+    def _():
+        acc[...] += term(cols_ref[:half, :], far_lo_ref[...]) + term(
+            cols_ref[half:, :], far_hi_ref[...]
+        )
+
+    @pl.when(slot == 3)
+    def _():
+        out_ref[...] = (acc[...] + term(cols_ref[...], right_ref[...])).astype(out_ref.dtype)
+
+
+def weight_block(cols, ctx_parts):
+    slots, tokens, rows = cols.shape
+    width = ctx_parts[0].shape[1]
+    full = pl.BlockSpec((tokens, width), lambda s: (0, 0))
+    half = pl.BlockSpec((tokens // 2, width), lambda s: (0, 0))
+    return pl.pallas_call(
+        wgrad_kernel,
+        out_shape=jax.ShapeDtypeStruct((rows, width), jnp.bfloat16),
+        grid=(slots,),
+        in_specs=[
+            pl.BlockSpec((None, tokens, rows), lambda s: (s, 0, 0)),
+            full,
+            full,
+            half,
+            half,
+            full,
+        ],
+        out_specs=pl.BlockSpec((rows, width), lambda s: (0, 0)),
+        scratch_shapes=[pltpu.VMEM((rows, width), jnp.float32)],
+        compiler_params=pltpu.CompilerParams(
+            dimension_semantics=("arbitrary",), vmem_limit_bytes=48 * 1024 * 1024
+        ),
+        cost_estimate=pl.CostEstimate(
+            flops=2 * slots * tokens * rows * width,
+            transcendentals=0,
+            bytes_accessed=2 * slots * tokens * (rows + width) + 2 * rows * width,
+        ),
+    )(cols, *ctx_parts)
+
+
 def on_device(queries, key_heads, value_heads, context_grad, output_grad, random_blocks):
     dp_count = lax.axis_size("dp")
     dp_pos = lax.axis_index("dp")
+    pipe_count = lax.axis_size("pipe")
+    pipe_pos = lax.axis_index("pipe")
+    upper_half = (pipe_pos >= pipe_count // 2).astype(jnp.int32)
     rows_here = output_grad.shape[2]
     width_model = output_grad.shape[3]
     quarter = width_model // (2 * dp_count)
-    pieces = output_grad[0, 0].reshape(rows_here, 2, dp_count, quarter).transpose(2, 0, 1, 3)
-    received = [None] * dp_count
-    received_own = lax.dynamic_index_in_dim(pieces, dp_pos, 0, keepdims=False)
+    pieces = output_grad[0, 0].reshape(rows_here, 2, dp_count, quarter).transpose(2, 1, 0, 3)
+    received = [lax.dynamic_index_in_dim(pieces, dp_pos, 0, keepdims=False)]
     for shift in range(1, dp_count):
         target = (dp_pos + shift) % dp_count
         outgoing = lax.dynamic_index_in_dim(pieces, target, 0, keepdims=False)
-        received[shift] = shift_over(outgoing, "dp", shift)
-    received[0] = received_own
-    moved_cols = jnp.stack(received)
-    columns = lax.all_gather(moved_cols, "tensor", axis=1, tiled=True)
+        received.append(shift_over(outgoing, "dp", shift))
+    moved = jnp.stack(received)
+    send_cols = lax.dynamic_index_in_dim(moved, 1 - upper_half, 1, keepdims=False)
+    keep_cols = lax.dynamic_index_in_dim(moved, upper_half, 1, keepdims=False)
+    send_all = lax.all_gather(send_cols, "tensor", axis=1, tiled=True)
+    keep_all = lax.all_gather(keep_cols, "tensor", axis=1, tiled=True)
 
     query_grad, key_grad, value_grad, ctx_rows = attention_backward(
         queries[0, 0], key_heads[0, 0], value_heads[0, 0], context_grad[0, 0], random_blocks
     )
-    tokens_all, width_here = ctx_rows.shape
-    ctx_parts = [None] * dp_count
-    ctx_parts[0] = ctx_rows
-    for shift in range(1, dp_count):
-        ctx_parts[shift] = shift_over(ctx_rows, "dp", shift)
-    contexts = jnp.stack(ctx_parts)
-
-    summed = lax.dot_general(
-        columns.reshape(dp_count * tokens_all, 2 * quarter),
-        contexts.reshape(dp_count * tokens_all, width_here),
-        (((0,), (0,)), ((), ())),
-        preferred_element_type=jnp.float32,
-    ).reshape(2, quarter, width_here)
-    summed_b = summed.astype(jnp.bfloat16)
-    pipe_count = lax.axis_size("pipe")
-    pipe_pos = lax.axis_index("pipe")
-    upper_half = (pipe_pos >= pipe_count // 2).astype(jnp.int32)
-    own_half = lax.dynamic_index_in_dim(summed_b, upper_half, 0, keepdims=False)
-    outgoing = lax.dynamic_index_in_dim(summed_b, 1 - upper_half, 0, keepdims=False)
+    tokens_all = ctx_rows.shape[0]
+    split = tokens_all // 2
+    from_left = shift_over(ctx_rows, "dp", 1)
+    from_right = shift_over(ctx_rows, "dp", -1)
+    far_lo = shift_over(from_left[:split], "dp", 1)
+    far_hi = shift_over(from_right[split:], "dp", -1)
+    ctx_parts = (ctx_rows, from_left, far_lo, far_hi, from_right)
+
+    send_block = weight_block(send_all, ctx_parts)
     incoming = lax.ppermute(
-        outgoing, "pipe", [(i, pipe_count - 1 - i) for i in range(pipe_count)]
-    )
-    weight_grad = (own_half.astype(jnp.float32) + incoming.astype(jnp.float32)).astype(
+        send_block, "pipe", [(i, pipe_count - 1 - i) for i in range(pipe_count)]
+    )
+    keep_block = weight_block(keep_all, ctx_parts)
+    weight_grad = (keep_block.astype(jnp.float32) + incoming.astype(jnp.float32)).astype(
         jnp.bfloat16
     )[None]
     shape4 = queries.shape

time: 299 us -> 232 us (0.78)
  local copies, waits for them, and re-layouts: 54.8 us -> 12.6 us
  waiting for transfers between devices: 153 us -> 129 us
  Pallas kernels: 37.8 us -> 54.3 us
  matrix products: 14.7 us -> 0 us
  other arithmetic: 9.12 us -> 2.76 us
  starting transfers between devices: 14.1 us -> 18.4 us
    ppermute x1, waiting for transfers between devices: 50.9 us -> 0.01 us  [on_device(): lax.ppermute(send_block, 'pipe', [(i, pipe_count - 1 - i) for i in range(...]
    all_gather x1 -> x2, waiting for transfers between devices: 19.7 us -> 58.5 us  [the longest x1 58.5 us: on_device(): keep_all = lax.all_gather(keep_cols, 'tensor', axis=1, tiled=True)]
    all_gather x1 -> x0, local copies, waits for them, and re-layouts: 23.1 us -> none  [on_device(): columns = lax.all_gather(moved_cols, 'tensor', axis=1, tiled=True)]
    dot_general x1 -> x0, local copies, waits for them, and re-layouts: 16.6 us -> none  [on_device(): lax.dot_general(columns.reshape(dp_count * tokens_all, 2 * quarter), cont...]
    pallas_call x0 -> x2, Pallas kernels: none -> 16.6 us  [weight_block(): pl.pallas_call(wgrad_kernel, out_shape=jax.ShapeDtypeStruct((rows, width)...]
    dot_general x1 -> x0, matrix products: 14.7 us -> none  [on_device(): lax.dot_general(columns.reshape(dp_count * tokens_all, 2 * quarter), cont...]
    ppermute x6 -> x7, waiting for transfers between devices: 82.7 us -> 69.4 us  [shift_over(): lax.ppermute(block, axis, [(i, (i + shift) % count) for i in range(count)])]
    another operation x2 -> x1, other arithmetic: 6.56 us -> 0.2 us  [on_device(): moved = jnp.stack(received)]
  transfers between devices with their start and end apart: 8 -> 10, of which waited for: 6 -> 6; matrix products, arithmetic and copies ran while one was open for 2% -> 0% of each run, Pallas kernels for 13% -> 24%
where the time goes in v1:
time: 232 us; the launch traced here: 231 us
  waiting for transfers between devices  129 us (56%)
  Pallas kernels  54.3 us (23%)
  starting transfers between devices  18.4 us (8%)
  between operations  14.3 us (6%)
  local copies, waits for them, and re-layouts  12.6 us (5%)
  other arithmetic  2.76 us (1%)
    ppermute x7, waiting for transfers between devices, shift_over(): lax.ppermute(block, axis, [(i, (i + shift) % count) for i in range(count)])  69.4 us
    all_gather x1, waiting for transfers between devices, on_device(): keep_all = lax.all_gather(keep_cols, 'tensor', axis=1, tiled=True)  58.5 us
    pallas_call x1, Pallas kernels, attention_backward(): call(rb_flat, queries, key_heads, value_heads, context_grad)  37.7 us
    pallas_call x2, Pallas kernels, weight_block(): pl.pallas_call(wgrad_kernel, out_shape=jax.ShapeDtypeStruct((rows, width)...  16.6 us
    unnamed x32, local copies, waits for them, and re-layouts  11 us
    ppermute x7, starting transfers between devices, shift_over(): lax.ppermute(block, axis, [(i, (i + shift) % count) for i in range(count)])  10.3 us
    ppermute x1, starting transfers between devices, on_device(): lax.ppermute(send_block, 'pipe', [(i, pipe_count - 1 - i) for i in range(...  8.04 us
  transfers between devices with their start and end apart: 10, of which 6 were waited for; matrix products, arithmetic and copies ran while one was open for 0% of the time, Pallas kernels for 24%

profile of v1, /device:TPU:1, one launch (start us, length us, event | category | flops | bytes accessed | tf_op | source)
XLA Modules:
  0.0 231.1 jit_solution(9238679349302973883)
XLA Ops:
  7.3 1.9 copy.14
  9.3 0.2 copy.22
  9.5 3.4 %collective-permute-start.2 = (bf16[2,128,768]{2,1,0:T(8,128)(2,1)S(1)}, bf16[2,128,768]{2,1,0:T(8,128)(2,1)S(1)}, u32[]{:S(2)}, u32[]{:S(2)}) collective-permute-start(bf16[2,128,768]{2,1,0:T(8,128)(2,1)S(1)} %bitcast.32), channel_id=1, source_target_pairs={{0,3},{1,0},{2,1},{3,2},{4,7},{5,4},{6,5},{7,6},{8,11},{9,8},{10,9... | collective-permute-start | bytes 1179656 | tf_op jit(solution)/shard_map/ppermute | solution.py:131
  12.9 0.2 copy.21
  13.1 0.6 collective-permute-start.1
  13.7 0.2 copy.20
  13.8 0.7 collective-permute-start
  14.5 0.2 copy.19
  14.7 8.9 %collective-permute-done.2 = bf16[2,128,768]{2,1,0:T(8,128)(2,1)S(1)} collective-permute-done((bf16[2,128,768]{2,1,0:T(8,128)(2,1)S(1)}, bf16[2,128,768]{2,1,0:T(8,128)(2,1)S(1)}, u32[]{:S(2)}, u32[]{:S(2)}) %collective-permute-start.2) | collective-permute-done | bytes 393248 | tf_op jit(solution)/shard_map/ppermute | solution.py:131
  23.6 0.8 collective-permute-done.1
  24.4 9.7 %collective-permute-done = bf16[2,128,768]{2,1,0:T(8,128)(2,1)S(1)} collective-permute-done((bf16[2,128,768]{2,1,0:T(8,128)(2,1)S(1)}, bf16[2,128,768]{2,1,0:T(8,128)(2,1)S(1)}, u32[]{:S(2)}, u32[]{:S(2)}) %collective-permute-start) | collective-permute-done | bytes 393248 | tf_op jit(solution)/shard_map/ppermute | solution.py:131
  34.1 0.2 pad_maximum_fusion
  34.3 1.3 constant_dynamic-slice_fusion.1
  35.7 0.7 all-gather.5.cloned.1.call-update
  36.7 0.4 copy-done
  37.1 37.7 %shard_map.93 = (bf16[1024,768]{1,0:T(8,128)(2,1)}, bf16[1024,768]{1,0:T(8,128)(2,1)S(1)}, bf16[1024,768]{1,0:T(8,128)(2,1)}, bf16[1024,768]{1,0:T(8,128)(2,1)}) custom-call(s32[252]{0:T(256)S(1)} %reshape.20.rb_ref, bf16[1024,768]{1,0:T(8,128)(2,1)S(1)} %bitcast.25, bf16[1024,768]{1,0:T(8,128)(2,1)S(1)} %bitcast.26, bf16[1024,768]{1,0:T(8,128)(2,1)} %bitcast.37, ...), custom_call_target="tpu_custom_call" | custom-call | flops 9663676416 | bytes 11010048 | tf_op jit(solution)/shard_map/pallas_call | solution.py:123
  74.9 2.7 %collective-permute-start.5 = (bf16[1024,768]{1,0:T(8,128)(2,1)S(1)}, bf16[1024,768]{1,0:T(8,128)(2,1)S(1)}, u32[]{:S(2)}, u32[]{:S(2)}) collective-permute-start(bf16[1024,768]{1,0:T(8,128)(2,1)S(1)} %get-tuple-element.11.own_ref), channel_id=1, source_target_pairs={{0,3},{1,0},{2,1},{3,2},{4,7},{5,4},{6,5},{7,6},{8,11},{9,8},{10,9... | collective-permute-start | bytes 4718600 | tf_op jit(solution)/shard_map/ppermute | solution.py:131
  77.5 34.0 %collective-permute-done.3.left_ref = bf16[1024,768]{1,0:T(8,128)(2,1)S(1)} collective-permute-done((bf16[1024,768]{1,0:T(8,128)(2,1)S(1)}, bf16[1024,768]{1,0:T(8,128)(2,1)S(1)}, u32[]{:S(2)}, u32[]{:S(2)}) %collective-permute-start.3) | collective-permute-done | bytes 1572896 | tf_op jit(solution)/shard_map/ppermute | solution.py:131
  111.8 2.9 %collective-permute-start.6 = (bf16[512,768]{1,0:T(8,128)(2,1)S(1)}, bf16[512,768]{1,0:T(8,128)(2,1)S(1)}, u32[]{:S(2)}, u32[]{:S(2)}) collective-permute-start(bf16[512,768]{1,0:T(8,128)(2,1)S(1)} %slice.9), channel_id=1, source_target_pairs={{0,3},{1,0},{2,1},{3,2},{4,7},{5,4},{6,5},{7,6},{8,11},{9,8},{10,9... | collective-permute-start | bytes 2359304 | tf_op jit(solution)/shard_map/ppermute | solution.py:131
  114.7 16.1 %collective-permute-done.4.far_lo_ref = bf16[512,768]{1,0:T(8,128)(2,1)S(1)} collective-permute-done((bf16[512,768]{1,0:T(8,128)(2,1)S(1)}, bf16[512,768]{1,0:T(8,128)(2,1)S(1)}, u32[]{:S(2)}, u32[]{:S(2)}) %collective-permute-start.4) | collective-permute-done | bytes 786464 | tf_op jit(solution)/shard_map/ppermute | solution.py:131
  130.7 0.9 copy-done.5
  131.6 0.9 copy-done.8
  132.6 1.4 copy-done.3
  134.0 1.1 copy-done.6
  135.1 1.1 copy-done.9
  136.2 8.9 %shard_map.95 = bf16[768,768]{1,0:T(8,128)(2,1)} custom-call(bf16[4,1024,768]{2,1,0:T(8,128)(2,1)} %bitcast.35, bf16[1024,768]{1,0:T(8,128)(2,1)S(1)} %copy-done.3, bf16[1024,768]{1,0:T(8,128)(2,1)S(1)} %collective-permute-done.3.left_ref, bf16[512,768]{1,0:T(8,128)(2,1)S(1)} %copy-done.6, bf16[512,768]{1,0:T(8,128)(2,1)S(1)} %copy-done.9, ...), custom_call_target="tpu_custom_call" | custom-call | flops 4831838208 | bytes 13762560 | tf_op jit(solution)/shard_map/pallas_call | solution.py:167
  145.1 8.0 %collective-permute-start.7 = (bf16[768,768]{1,0:T(8,128)(2,1)}, bf16[768,768]{1,0:T(8,128)(2,1)}, u32[]{:S(2)}, u32[]{:S(2)}) collective-permute-start(bf16[768,768]{1,0:T(8,128)(2,1)} %shard_map.95), channel_id=1, source_target_pairs={{0,224},{32,192},{64,160},{96,128},{128,96},{160,64},{192,32},{224... | collective-permute-start | bytes 3538952 | tf_op jit(solution)/shard_map/ppermute | solution.py:225
  153.1 58.5 %all-gather.5.cloned.1.call-done = bf16[4,1,1024,768]{3,2,0,1:T(8,128)(2,1)} async-done(((bf16[4,1,128,768]{3,2,0,1:T(8,128)(2,1)}), bf16[4,1,1024,768]{3,2,0,1:T(8,128)(2,1)}) %all-gather.5.cloned.1.call-update) | async-done | bytes 6291472 | tf_op jit(solution)/shard_map/all_gather | solution.py:211
  211.7 1.1 copy-done.7
  212.8 1.1 copy-done.10
  213.9 7.7 %shard_map.94 = bf16[768,768]{1,0:T(8,128)(2,1)S(1)} custom-call(bf16[4,1024,768]{2,1,0:T(8,128)(2,1)} %bitcast.36, bf16[1024,768]{1,0:T(8,128)(2,1)S(1)} %copy-done.4, bf16[1024,768]{1,0:T(8,128)(2,1)S(1)} %collective-permute-done.3.left_ref, bf16[512,768]{1,0:T(8,128)(2,1)S(1)} %copy-done.7, bf16[512,768]{1,0:T(8,128)(2,1)S(1)} %copy-done.10, ...), custom_call_target="tpu_custom_call" | custom-call | flops 4831838208 | bytes 13762560 | tf_op jit(solution)/shard_map/pallas_call | solution.py:167
  221.7 2.6 %fusion = bf16[1,768,768]{2,1,0:T(8,128)(2,1)} fusion(bf16[768,768]{1,0:T(8,128)(2,1)} %collective-permute-done.7, bf16[768,768]{1,0:T(8,128)(2,1)S(1)} %shard_map.94), kind=kLoop, calls=%fused_computation.2 | loop fusion | flops 2359296 | bytes 3538944 | tf_op jit(solution)/shard_map/broadcast_in_dim | solution.py:229
  (32 shorter events, 0.7 us)
Async XLA Ops:
  7.2 125.4 %all-gather.7.cloned.1.call-start = ((), (), s32[]{:S(2)}) async-start(), calls=%async_computation.1 | async-start | bytes 7077888 | tf_op jit(solution)/shard_map/all_gather | solution.py:210
  9.5 14.1 %collective-permute-start.2 = (bf16[2,128,768]{2,1,0:T(8,128)(2,1)S(1)}, bf16[2,128,768]{2,1,0:T(8,128)(2,1)S(1)}, u32[]{:S(2)}, u32[]{:S(2)}) collective-permute-start(bf16[2,128,768]{2,1,0:T(8,128)(2,1)S(1)} %bitcast.32), channel_id=1, source_target_pairs={{0,3},{1,0},{2,1},{3,2},{4,7},{5,4},{6,5},{7,6},{8,11},{9,8},{10,9... | collective-permute-start | bytes 1179656 | tf_op jit(solution)/shard_map/ppermute | solution.py:131
  13.1 11.4 %collective-permute-start.1 = (bf16[2,128,768]{2,1,0:T(8,128)(2,1)S(1)}, bf16[2,128,768]{2,1,0:T(8,128)(2,1)S(1)}, u32[]{:S(2)}, u32[]{:S(2)}) collective-permute-start(bf16[2,128,768]{2,1,0:T(8,128)(2,1)S(1)} %bitcast.33), channel_id=1, source_target_pairs={{0,2},{1,3},{2,0},{3,1},{4,6},{5,7},{6,4},{7,5},{8,10},{9,11},{10,... | collective-permute-start | bytes 1179656 | tf_op jit(solution)/shard_map/ppermute | solution.py:131
  13.8 20.3 %collective-permute-start = (bf16[2,128,768]{2,1,0:T(8,128)(2,1)S(1)}, bf16[2,128,768]{2,1,0:T(8,128)(2,1)S(1)}, u32[]{:S(2)}, u32[]{:S(2)}) collective-permute-start(bf16[2,128,768]{2,1,0:T(8,128)(2,1)S(1)} %bitcast.34), channel_id=1, source_target_pairs={{0,1},{1,2},{2,3},{3,0},{4,5},{5,6},{6,7},{7,4},{8,9},{9,10},{10,1... | collective-permute-start | bytes 1179656 | tf_op jit(solution)/shard_map/ppermute | solution.py:131
  34.3 2.1 copy-start.12
  34.3 2.3 %copy-start.1 = (bf16[1,1,1024,768]{3,2,1,0:T(8,128)(2,1)S(1)}, bf16[1,1,1024,768]{3,2,1,0:T(8,128)(2,1)}, u32[]{:S(2)}) copy-start(bf16[1,1,1024,768]{3,2,1,0:T(8,128)(2,1)} %param.7) | copy-start | bytes 4718596
  35.6 1.5 copy-start
  35.6 176.1 %all-gather.5.cloned.1.call-start = ((), (), s32[]{:S(2)}) async-start(), calls=%async_computation | async-start | bytes 7077888 | tf_op jit(solution)/shard_map/all_gather | solution.py:211
  74.9 36.9 %copy-start.2 = (bf16[1024,768]{1,0:T(8,128)(2,1)}, bf16[1024,768]{1,0:T(8,128)(2,1)S(1)}, u32[]{:S(2)}) copy-start(bf16[1024,768]{1,0:T(8,128)(2,1)S(1)} %get-tuple-element.11.own_ref) | copy-start | bytes 4718596
  74.9 36.7 %collective-permute-start.3 = (bf16[1024,768]{1,0:T(8,128)(2,1)S(1)}, bf16[1024,768]{1,0:T(8,128)(2,1)S(1)}, u32[]{:S(2)}, u32[]{:S(2)}) collective-permute-start(bf16[1024,768]{1,0:T(8,128)(2,1)S(1)} %get-tuple-element.11.own_ref), channel_id=1, source_target_pairs={{0,1},{1,2},{2,3},{3,0},{4,5},{5,6},{6,7},{7,4},{8,9},{9,10},{10,1... | collective-permute-start | bytes 4718600 | tf_op jit(solution)/shard_map/ppermute | solution.py:131
  74.9 36.8 %collective-permute-start.5 = (bf16[1024,768]{1,0:T(8,128)(2,1)S(1)}, bf16[1024,768]{1,0:T(8,128)(2,1)S(1)}, u32[]{:S(2)}, u32[]{:S(2)}) collective-permute-start(bf16[1024,768]{1,0:T(8,128)(2,1)S(1)} %get-tuple-element.11.own_ref), channel_id=1, source_target_pairs={{0,3},{1,0},{2,1},{3,2},{4,7},{5,4},{6,5},{7,6},{8,11},{9,8},{10,9... | collective-permute-start | bytes 4718600 | tf_op jit(solution)/shard_map/ppermute | solution.py:131
  111.6 19.1 %collective-permute-start.4 = (bf16[512,768]{1,0:T(8,128)(2,1)S(1)}, bf16[512,768]{1,0:T(8,128)(2,1)S(1)}, u32[]{:S(2)}, u32[]{:S(2)}) collective-permute-start(bf16[512,768]{1,0:T(8,128)(2,1)S(1)} %slice.8), channel_id=1, source_target_pairs={{0,1},{1,2},{2,3},{3,0},{4,5},{5,6},{6,7},{7,4},{8,9},{9,10},{10,1... | collective-permute-start | bytes 2359304 | tf_op jit(solution)/shard_map/ppermute | solution.py:131
  111.7 19.0 %copy-start.11 = (bf16[1024,768]{1,0:T(8,128)(2,1)}, bf16[1024,768]{1,0:T(8,128)(2,1)S(1)}, u32[]{:S(2)}) copy-start(bf16[1024,768]{1,0:T(8,128)(2,1)S(1)} %collective-permute-done.5.right_ref) | copy-start | bytes 4718596
  111.8 19.9 %collective-permute-start.6 = (bf16[512,768]{1,0:T(8,128)(2,1)S(1)}, bf16[512,768]{1,0:T(8,128)(2,1)S(1)}, u32[]{:S(2)}, u32[]{:S(2)}) collective-permute-start(bf16[512,768]{1,0:T(8,128)(2,1)S(1)} %slice.9), channel_id=1, source_target_pairs={{0,3},{1,0},{2,1},{3,2},{4,7},{5,4},{6,5},{7,6},{8,11},{9,8},{10,9... | collective-permute-start | bytes 2359304 | tf_op jit(solution)/shard_map/ppermute | solution.py:131
  130.7 0.9 copy-start.5
  131.6 0.9 copy-start.8
  132.6 1.4 copy-start.3
  134.0 1.1 copy-start.6
  135.1 1.1 copy-start.9
  136.2 75.4 %copy-start.4 = (bf16[1024,768]{1,0:T(8,128)(2,1)S(1)}, bf16[1024,768]{1,0:T(8,128)(2,1)}, u32[]{:S(2)}) copy-start(bf16[1024,768]{1,0:T(8,128)(2,1)} %copy-done.2) | copy-start | bytes 4718596
  145.1 76.6 %collective-permute-start.7 = (bf16[768,768]{1,0:T(8,128)(2,1)}, bf16[768,768]{1,0:T(8,128)(2,1)}, u32[]{:S(2)}, u32[]{:S(2)}) collective-permute-start(bf16[768,768]{1,0:T(8,128)(2,1)} %shard_map.95), channel_id=1, source_target_pairs={{0,224},{32,192},{64,160},{96,128},{128,96},{160,64},{192,32},{224... | collective-permute-start | bytes 3538952 | tf_op jit(solution)/shard_map/ppermute | solution.py:225
  211.7 1.1 copy-start.7
  212.8 1.1 copy-start.10
Sparse Core Ops, SparseCore 0:
  35.7 75.2 all-gather.6
  112.8 98.8 all-gather.4

commit v2 on v1

--- a/solution.py
+++ b/solution.py
@@ -131,7 +131,9 @@
     return lax.ppermute(block, axis, [(i, (i + shift) % count) for i in range(count)])
 
 
-def wgrad_kernel(cols_ref, own_ref, left_ref, far_lo_ref, far_hi_ref, right_ref, out_ref, acc):
+def wgrad_kernel(
+    cols0_ref, cols_ref, own_ref, left_ref, far_lo_ref, far_hi_ref, right_ref, out_ref, acc
+):
     slot = pl.program_id(0)
     half = far_lo_ref.shape[0]
 
@@ -142,7 +144,7 @@
 
     @pl.when(slot == 0)
     def _():
-        acc[...] = term(cols_ref[...], own_ref[...])
+        acc[...] = term(cols0_ref[...], own_ref[...])
 
     @pl.when(slot == 1)
     def _():
@@ -159,17 +161,18 @@
         out_ref[...] = (acc[...] + term(cols_ref[...], right_ref[...])).astype(out_ref.dtype)
 
 
-def weight_block(cols, ctx_parts):
-    slots, tokens, rows = cols.shape
+def weight_block(cols0, cols, ctx_parts):
+    others, tokens, rows = cols.shape
     width = ctx_parts[0].shape[1]
     full = pl.BlockSpec((tokens, width), lambda s: (0, 0))
     half = pl.BlockSpec((tokens // 2, width), lambda s: (0, 0))
     return pl.pallas_call(
         wgrad_kernel,
         out_shape=jax.ShapeDtypeStruct((rows, width), jnp.bfloat16),
-        grid=(slots,),
+        grid=(others + 1,),
         in_specs=[
-            pl.BlockSpec((None, tokens, rows), lambda s: (s, 0, 0)),
+            pl.BlockSpec((tokens, rows), lambda s: (0, 0)),
+            pl.BlockSpec((None, tokens, rows), lambda s: (jnp.maximum(s - 1, 0), 0, 0)),
             full,
             full,
             half,
@@ -182,11 +185,35 @@
             dimension_semantics=("arbitrary",), vmem_limit_bytes=48 * 1024 * 1024
         ),
         cost_estimate=pl.CostEstimate(
-            flops=2 * slots * tokens * rows * width,
+            flops=2 * (others + 1) * tokens * rows * width,
             transcendentals=0,
-            bytes_accessed=2 * slots * tokens * (rows + width) + 2 * rows * width,
-        ),
-    )(cols, *ctx_parts)
+            bytes_accessed=2 * (others + 1) * tokens * (rows + width) + 2 * rows * width,
+        ),
+    )(cols0, cols, *ctx_parts)
+
+
+def gather_over_tensor(piece, tokens_all):
+    count = lax.axis_size("tensor")
+    pos = lax.axis_index("tensor")
+    along_y = 4 if count % 4 == 0 else count
+    along_z = count // along_y
+    rows = piece.shape[1]
+    out = jnp.zeros((piece.shape[0], tokens_all, piece.shape[2]), piece.dtype)
+    out = lax.dynamic_update_slice(out, piece, (0, pos * rows, 0))
+    zl = pos // along_y
+    y = pos % along_y
+    for dz in range(along_z):
+        for dy in range(along_y):
+            if dz == 0 and dy == 0:
+                continue
+            route = [
+                (t, ((t // along_y + dz) % along_z) * along_y + (t % along_y + dy) % along_y)
+                for t in range(count)
+            ]
+            got = lax.ppermute(piece, "tensor", route)
+            src = ((zl - dz) % along_z) * along_y + (y - dy) % along_y
+            out = lax.dynamic_update_slice(out, got, (0, src * rows, 0))
+    return out
 
 
 def on_device(queries, key_heads, value_heads, context_grad, output_grad, random_blocks):
@@ -199,16 +226,17 @@
     width_model = output_grad.shape[3]
     quarter = width_model // (2 * dp_count)
     pieces = output_grad[0, 0].reshape(rows_here, 2, dp_count, quarter).transpose(2, 1, 0, 3)
-    received = [lax.dynamic_index_in_dim(pieces, dp_pos, 0, keepdims=False)]
+    pieces = jnp.where(upper_half == 1, pieces, pieces[:, ::-1])
+    own_piece = lax.dynamic_index_in_dim(pieces, dp_pos, 0, keepdims=False)
+    slot0 = gather_over_tensor(own_piece, output_grad.shape[2] * lax.axis_size("tensor"))
+    received = []
     for shift in range(1, dp_count):
         target = (dp_pos + shift) % dp_count
         outgoing = lax.dynamic_index_in_dim(pieces, target, 0, keepdims=False)
         received.append(shift_over(outgoing, "dp", shift))
     moved = jnp.stack(received)
-    send_cols = lax.dynamic_index_in_dim(moved, 1 - upper_half, 1, keepdims=False)
-    keep_cols = lax.dynamic_index_in_dim(moved, upper_half, 1, keepdims=False)
-    send_all = lax.all_gather(send_cols, "tensor", axis=1, tiled=True)
-    keep_all = lax.all_gather(keep_cols, "tensor", axis=1, tiled=True)
+    send_all = lax.all_gather(moved[:, 0], "tensor", axis=1, tiled=True)
+    keep_all = lax.all_gather(moved[:, 1], "tensor", axis=1, tiled=True)
 
     query_grad, key_grad, value_grad, ctx_rows = attention_backward(
         queries[0, 0], key_heads[0, 0], value_heads[0, 0], context_grad[0, 0], random_blocks
@@ -221,11 +249,11 @@
     far_hi = shift_over(from_right[split:], "dp", -1)
     ctx_parts = (ctx_rows, from_left, far_lo, far_hi, from_right)
 
-    send_block = weight_block(send_all, ctx_parts)
+    send_block = weight_block(slot0[0], send_all, ctx_parts)
     incoming = lax.ppermute(
         send_block, "pipe", [(i, pipe_count - 1 - i) for i in range(pipe_count)]
     )
-    keep_block = weight_block(keep_all, ctx_parts)
+    keep_block = weight_block(slot0[1], keep_all, ctx_parts)
     weight_grad = (keep_block.astype(jnp.float32) + incoming.astype(jnp.float32)).astype(
         jnp.bfloat16
     )[None]

time: 232 us -> 257 us (1.11)
  the two profiles are of different devices: /device:TPU:1 before, /device:TPU:49 now
where the time goes in v2:
time: 257 us; the launch traced here: 256 us
  waiting for transfers between devices  132 us (51%)
  Pallas kernels  56.1 us (22%)
  local copies, waits for them, and re-layouts  27.2 us (11%)
  starting transfers between devices  24.8 us (10%)
  between operations  14.3 us (6%)
    ppermute x7, waiting for transfers between devices, gather_over_tensor(): got = lax.ppermute(piece, 'tensor', route)  70.9 us
    ppermute x1, waiting for transfers between devices, on_device(): lax.ppermute(send_block, 'pipe', [(i, pipe_count - 1 - i) for i in range(...  39.3 us
    pallas_call x1, Pallas kernels, attention_backward(): call(rb_flat, queries, key_heads, value_heads, context_grad)  37.7 us
    ppermute x7, waiting for transfers between devices, shift_over(): lax.ppermute(block, axis, [(i, (i + shift) % count) for i in range(count)])  19.8 us
    pallas_call x2, Pallas kernels, weight_block(): pl.pallas_call(wgrad_kernel, out_shape=jax.ShapeDtypeStruct((rows, width)...  18.4 us
    dynamic_update_slice x7, local copies, waits for them, and re-layouts, gather_over_tensor(): out = lax.dynamic_update_slice(out, got, (0, src * rows, 0))  9.49 us
    ppermute x7, starting transfers between devices, shift_over(): lax.ppermute(block, axis, [(i, (i + shift) % count) for i in range(count)])  9.19 us
    ppermute x7, starting transfers between devices, gather_over_tensor(): got = lax.ppermute(piece, 'tensor', route)  8.87 us
  transfers between devices with their start and end apart: 17, of which 9 were waited for; matrix products, arithmetic and copies ran while one was open for 6% of the time, Pallas kernels for 22%

profile of v2, /device:TPU:49, one launch (start us, length us, event | category | flops | bytes accessed | tf_op | source)
XLA Modules:
  0.0 256.1 jit_solution(13562303487157197329)
XLA Ops:
  7.2 3.6 %reshape_squeeze.3 = bf16[128,2,4,768]{3,2,1,0:T(4,128)(2,1)S(1)} reshape(bf16[1,1,128,6144]{3,2,1,0:T(8,128)(2,1)} %param.10) | data formatting | bytes 3145728 | tf_op jit(solution)/shard_map/reshape;squeeze | solution.py:228
  11.6 2.6 collective-permute-start.9
  15.2 7.5 %collective-permute-done.9 = bf16[2,128,768]{2,1,0:T(8,128)(2,1)S(1)} collective-permute-done((bf16[2,128,768]{2,1,0:T(8,128)(2,1)S(1)}, bf16[2,128,768]{2,1,0:T(8,128)(2,1)S(1)}, u32[]{:S(2)}, u32[]{:S(2)}) %collective-permute-start.9) | collective-permute-done | bytes 393248 | tf_op jit(solution)/shard_map/ppermute | solution.py:131
  22.7 2.7 %collective-permute-done.8 = bf16[2,128,768]{2,1,0:T(8,128)(2,1)S(1)} collective-permute-done((bf16[2,128,768]{2,1,0:T(8,128)(2,1)S(1)}, bf16[2,128,768]{2,1,0:T(8,128)(2,1)S(1)}, u32[]{:S(2)}, u32[]{:S(2)}) %collective-permute-start.8) | collective-permute-done | bytes 393248 | tf_op jit(solution)/shard_map/ppermute | solution.py:131
  25.4 9.7 %collective-permute-done.7 = bf16[2,128,768]{2,1,0:T(8,128)(2,1)S(1)} collective-permute-done((bf16[2,128,768]{2,1,0:T(8,128)(2,1)S(1)}, bf16[2,128,768]{2,1,0:T(8,128)(2,1)S(1)}, u32[]{:S(2)}, u32[]{:S(2)}) %collective-permute-start.7) | collective-permute-done | bytes 393248 | tf_op jit(solution)/shard_map/ppermute | solution.py:131
  37.5 37.7 %shard_map.93 = (bf16[1024,768]{1,0:T(8,128)(2,1)}, bf16[1024,768]{1,0:T(8,128)(2,1)}, bf16[1024,768]{1,0:T(8,128)(2,1)}, bf16[1024,768]{1,0:T(8,128)(2,1)}) custom-call(s32[252]{0:T(256)S(1)} %reshape.20.rb_ref, bf16[1024,768]{1,0:T(8,128)(2,1)S(1)} %bitcast.32, bf16[1024,768]{1,0:T(8,128)(2,1)S(1)} %bitcast.33, bf16[1024,768]{1,0:T(8,128)(2,1)} %bitcast.40, ...), custom_call_target="tpu_custom_call" | custom-call | flops 9663676416 | bytes 11010048 | tf_op jit(solution)/shard_map/pallas_call | solution.py:123
  75.2 2.7 %collective-permute-start.12 = (bf16[1024,768]{1,0:T(8,128)(2,1)}, bf16[1024,768]{1,0:T(8,128)(2,1)S(1)}, u32[]{:S(2)}, u32[]{:S(2)}) collective-permute-start(bf16[1024,768]{1,0:T(8,128)(2,1)} %get-tuple-element.11.own_ref), channel_id=1, source_target_pairs={{0,3},{1,0},{2,1},{3,2},{4,7},{5,4},{6,5},{7,6},{8,11},{9,8},{10,9... | collective-permute-start | bytes 4718600 | tf_op jit(solution)/shard_map/ppermute | solution.py:131
  77.9 1.9 broadcast_in_dim.6
  79.8 1.8 constant_dynamic-update-slice_fusion.7
  83.8 17.1 %collective-permute-done = bf16[2,128,768]{2,1,0:T(8,128)(2,1)} collective-permute-done((bf16[2,128,768]{2,1,0:T(8,128)(2,1)S(1)}, bf16[2,128,768]{2,1,0:T(8,128)(2,1)}, u32[]{:S(2)}, u32[]{:S(2)}) %collective-permute-start) | collective-permute-done | bytes 393248 | tf_op jit(solution)/shard_map/ppermute | solution.py:213
  100.9 8.7 %collective-permute-done.1 = bf16[2,128,768]{2,1,0:T(8,128)(2,1)} collective-permute-done((bf16[2,128,768]{2,1,0:T(8,128)(2,1)S(1)}, bf16[2,128,768]{2,1,0:T(8,128)(2,1)}, u32[]{:S(2)}, u32[]{:S(2)}) %collective-permute-start.1) | collective-permute-done | bytes 393248 | tf_op jit(solution)/shard_map/ppermute | solution.py:213
  110.6 1.8 constant_dynamic-update-slice_fusion.6
  112.3 2.8 %collective-permute-start.5 = (bf16[2,128,768]{2,1,0:T(8,128)(2,1)S(1)}, bf16[2,128,768]{2,1,0:T(8,128)(2,1)S(1)}, u32[]{:S(2)}, u32[]{:S(2)}) collective-permute-start(bf16[2,128,768]{2,1,0:T(8,128)(2,1)S(1)} %get-tuple-element.13), channel_id=1, source_target_pairs={{0,24},{4,28},{8,16},{12,20},{16,8},{20,12},{24,0},{28,4},{1,25},{... | collective-permute-start | bytes 1179656 | tf_op jit(solution)/shard_map/ppermute | solution.py:213
  115.1 1.8 constant_dynamic-update-slice_fusion.5
  116.9 2.9 %collective-permute-start.6 = (bf16[2,128,768]{2,1,0:T(8,128)(2,1)S(1)}, bf16[2,128,768]{2,1,0:T(8,128)(2,1)S(1)}, u32[]{:S(2)}, u32[]{:S(2)}) collective-permute-start(bf16[2,128,768]{2,1,0:T(8,128)(2,1)S(1)} %get-tuple-element.13), channel_id=1, source_target_pairs={{0,28},{4,16},{8,20},{12,24},{16,12},{20,0},{24,4},{28,8},{1,29},{... | collective-permute-start | bytes 1179656 | tf_op jit(solution)/shard_map/ppermute | solution.py:213
  119.8 1.8 constant_dynamic-update-slice_fusion.4
  121.7 1.3 collective-permute-start.11
  123.1 1.6 collective-permute-start.13
  124.6 1.8 constant_dynamic-update-slice_fusion.3
  127.2 21.3 %collective-permute-done.5 = bf16[2,128,768]{2,1,0:T(8,128)(2,1)S(1)} collective-permute-done((bf16[2,128,768]{2,1,0:T(8,128)(2,1)S(1)}, bf16[2,128,768]{2,1,0:T(8,128)(2,1)S(1)}, u32[]{:S(2)}, u32[]{:S(2)}) %collective-permute-start.5) | collective-permute-done | bytes 393248 | tf_op jit(solution)/shard_map/ppermute | solution.py:213
  149.2 23.9 %collective-permute-done.6 = bf16[2,128,768]{2,1,0:T(8,128)(2,1)S(1)} collective-permute-done((bf16[2,128,768]{2,1,0:T(8,128)(2,1)S(1)}, bf16[2,128,768]{2,1,0:T(8,128)(2,1)S(1)}, u32[]{:S(2)}, u32[]{:S(2)}) %collective-permute-start.6) | collective-permute-done | bytes 393248 | tf_op jit(solution)/shard_map/ppermute | solution.py:213
  173.9 2.1 slice_bitcast_fusion.1
  177.8 1.1 copy-done.3
  178.9 1.1 copy-done.6
  180.1 9.7 %shard_map.95 = bf16[768,768]{1,0:T(8,128)(2,1)} custom-call(bf16[1024,768]{1,0:T(8,128)(2,1)S(1)} %get-tuple-element.15.cols0_ref, bf16[3,1024,768]{2,1,0:T(8,128)(2,1)} %bitcast.39, bf16[1024,768]{1,0:T(8,128)(2,1)} %get-tuple-element.11.own_ref, bf16[1024,768]{1,0:T(8,128)(2,1)} %copy-done.9, bf16[512,768]{1,0:T(8,128)(2,1)S(1)} %copy-done.3, ...), custom_call_target="tpu_custom_call" | custom-call | flops 4831838208 | bytes 13762560 | tf_op jit(solution)/shard_map/pallas_call | solution.py:169
  189.8 6.7 %collective-permute-start.14 = (bf16[768,768]{1,0:T(8,128)(2,1)}, bf16[768,768]{1,0:T(8,128)(2,1)S(1)}, u32[]{:S(2)}, u32[]{:S(2)}) collective-permute-start(bf16[768,768]{1,0:T(8,128)(2,1)} %shard_map.95), channel_id=1, source_target_pairs={{0,224},{32,192},{64,160},{96,128},{128,96},{160,64},{192,32},{224... | collective-permute-start | bytes 3538952 | tf_op jit(solution)/shard_map/ppermute | solution.py:253
  196.5 1.2 all-gather.5.cloned.1.call-done
  197.7 1.1 copy-done.4
  198.8 1.1 copy-done.7
  199.9 8.7 %shard_map.94 = bf16[768,768]{1,0:T(8,128)(2,1)S(1)} custom-call(bf16[1024,768]{1,0:T(8,128)(2,1)S(1)} %get-tuple-element.14.cols0_ref, bf16[3,1024,768]{2,1,0:T(8,128)(2,1)} %bitcast.38, bf16[1024,768]{1,0:T(8,128)(2,1)} %get-tuple-element.11.own_ref, bf16[1024,768]{1,0:T(8,128)(2,1)} %copy-done.9, bf16[512,768]{1,0:T(8,128)(2,1)S(1)} %copy-done.4, ...), custom_call_target="tpu_custom_call" | custom-call | flops 4831838208 | bytes 13762560 | tf_op jit(solution)/shard_map/pallas_call | solution.py:169
  208.6 39.3 %collective-permute-done.14 = bf16[768,768]{1,0:T(8,128)(2,1)S(1)} collective-permute-done((bf16[768,768]{1,0:T(8,128)(2,1)}, bf16[768,768]{1,0:T(8,128)(2,1)S(1)}, u32[]{:S(2)}, u32[]{:S(2)}) %collective-permute-start.14) | collective-permute-done | bytes 1179680 | tf_op jit(solution)/shard_map/ppermute | solution.py:253
  247.9 1.3 fusion
  (52 shorter events, 11.6 us)
Async XLA Ops:
  7.2 170.6 %all-gather.7.cloned.1.call-start = ((), (), s32[]{:S(2)}) async-start(), calls=%async_computation.1 | async-start | bytes 5308416 | tf_op jit(solution)/shard_map/all_gather | solution.py:238
  11.4 23.6 %copy-start.8 = (bf16[4,2,128,768]{3,2,1,0:T(8,128)(2,1)}, bf16[4,2,128,768]{3,2,1,0:T(8,128)(2,1)S(1)}, u32[]{:S(2)}) copy-start(bf16[4,2,128,768]{3,2,1,0:T(8,128)(2,1)S(1)} %reverse_select_fusion) | copy-start | bytes 4718596
  11.6 11.2 %collective-permute-start.9 = (bf16[2,128,768]{2,1,0:T(8,128)(2,1)S(1)}, bf16[2,128,768]{2,1,0:T(8,128)(2,1)S(1)}, u32[]{:S(2)}, u32[]{:S(2)}) collective-permute-start(bf16[2,128,768]{2,1,0:T(8,128)(2,1)S(1)} %get-tuple-element.17), channel_id=1, source_target_pairs={{0,3},{1,0},{2,1},{3,2},{4,7},{5,4},{6,5},{7,6},{8,11},{9,8},{10,9... | collective-permute-start | bytes 1179656 | tf_op jit(solution)/shard_map/ppermute | solution.py:131
  14.1 11.3 %collective-permute-start.8 = (bf16[2,128,768]{2,1,0:T(8,128)(2,1)S(1)}, bf16[2,128,768]{2,1,0:T(8,128)(2,1)S(1)}, u32[]{:S(2)}, u32[]{:S(2)}) collective-permute-start(bf16[2,128,768]{2,1,0:T(8,128)(2,1)S(1)} %get-tuple-element.18), channel_id=1, source_target_pairs={{0,2},{1,3},{2,0},{3,1},{4,6},{5,7},{6,4},{7,5},{8,10},{9,11},{10,... | collective-permute-start | bytes 1179656 | tf_op jit(solution)/shard_map/ppermute | solution.py:131
  14.6 20.4 %collective-permute-start.7 = (bf16[2,128,768]{2,1,0:T(8,128)(2,1)S(1)}, bf16[2,128,768]{2,1,0:T(8,128)(2,1)S(1)}, u32[]{:S(2)}, u32[]{:S(2)}) collective-permute-start(bf16[2,128,768]{2,1,0:T(8,128)(2,1)S(1)} %get-tuple-element.16), channel_id=1, source_target_pairs={{0,1},{1,2},{2,3},{3,0},{4,5},{5,6},{6,7},{7,4},{8,9},{9,10},{10,1... | collective-permute-start | bytes 1179656 | tf_op jit(solution)/shard_map/ppermute | solution.py:131
  35.2 1.9 copy-start.11
  35.2 2.2 copy-start
  35.2 2.3 copy-start.1
  36.4 161.3 %all-gather.5.cloned.1.call-start = ((), (), s32[]{:S(2)}) async-start(), calls=%async_computation | async-start | bytes 5308416 | tf_op jit(solution)/shard_map/all_gather | solution.py:239
  75.2 41.7 %collective-permute-start.10 = (bf16[1024,768]{1,0:T(8,128)(2,1)}, bf16[1024,768]{1,0:T(8,128)(2,1)S(1)}, u32[]{:S(2)}, u32[]{:S(2)}) collective-permute-start(bf16[1024,768]{1,0:T(8,128)(2,1)} %get-tuple-element.11.own_ref), channel_id=1, source_target_pairs={{0,1},{1,2},{2,3},{3,0},{4,5},{5,6},{6,7},{7,4},{8,9},{9,10},{10,1... | collective-permute-start | bytes 4718600 | tf_op jit(solution)/shard_map/ppermute | solution.py:131
  75.2 46.5 %collective-permute-start.12 = (bf16[1024,768]{1,0:T(8,128)(2,1)}, bf16[1024,768]{1,0:T(8,128)(2,1)S(1)}, u32[]{:S(2)}, u32[]{:S(2)}) collective-permute-start(bf16[1024,768]{1,0:T(8,128)(2,1)} %get-tuple-element.11.own_ref), channel_id=1, source_target_pairs={{0,3},{1,0},{2,1},{3,2},{4,7},{5,4},{6,5},{7,6},{8,11},{9,8},{10,9... | collective-permute-start | bytes 4718600 | tf_op jit(solution)/shard_map/ppermute | solution.py:131
  81.6 19.3 %collective-permute-start = (bf16[2,128,768]{2,1,0:T(8,128)(2,1)S(1)}, bf16[2,128,768]{2,1,0:T(8,128)(2,1)}, u32[]{:S(2)}, u32[]{:S(2)}) collective-permute-start(bf16[2,128,768]{2,1,0:T(8,128)(2,1)S(1)} %get-tuple-element.13), channel_id=1, source_target_pairs={{0,4},{4,8},{8,12},{12,0},{16,20},{20,24},{24,28},{28,16},{1,5},{5... | collective-permute-start | bytes 1179656 | tf_op jit(solution)/shard_map/ppermute | solution.py:213
  82.6 27.0 %collective-permute-start.1 = (bf16[2,128,768]{2,1,0:T(8,128)(2,1)S(1)}, bf16[2,128,768]{2,1,0:T(8,128)(2,1)}, u32[]{:S(2)}, u32[]{:S(2)}) collective-permute-start(bf16[2,128,768]{2,1,0:T(8,128)(2,1)S(1)} %get-tuple-element.13), channel_id=1, source_target_pairs={{0,8},{4,12},{8,0},{12,4},{16,24},{20,28},{24,16},{28,20},{1,9},{5... | collective-permute-start | bytes 1179656 | tf_op jit(solution)/shard_map/ppermute | solution.py:213
  83.0 29.4 %collective-permute-start.2 = (bf16[2,128,768]{2,1,0:T(8,128)(2,1)S(1)}, bf16[2,128,768]{2,1,0:T(8,128)(2,1)}, u32[]{:S(2)}, u32[]{:S(2)}) collective-permute-start(bf16[2,128,768]{2,1,0:T(8,128)(2,1)S(1)} %get-tuple-element.13), channel_id=1, source_target_pairs={{0,12},{4,0},{8,4},{12,8},{16,28},{20,16},{24,20},{28,24},{1,13},{... | collective-permute-start | bytes 1179656 | tf_op jit(solution)/shard_map/ppermute | solution.py:213
  100.9 22.1 %collective-permute-start.3 = (bf16[2,128,768]{2,1,0:T(8,128)(2,1)S(1)}, bf16[2,128,768]{2,1,0:T(8,128)(2,1)}, u32[]{:S(2)}, u32[]{:S(2)}) collective-permute-start(bf16[2,128,768]{2,1,0:T(8,128)(2,1)S(1)} %get-tuple-element.13), channel_id=1, source_target_pairs={{0,16},{4,20},{8,24},{12,28},{16,0},{20,4},{24,8},{28,12},{1,17},{... | collective-permute-start | bytes 1179656 | tf_op jit(solution)/shard_map/ppermute | solution.py:213
  109.6 16.8 %collective-permute-start.4 = (bf16[2,128,768]{2,1,0:T(8,128)(2,1)S(1)}, bf16[2,128,768]{2,1,0:T(8,128)(2,1)S(1)}, u32[]{:S(2)}, u32[]{:S(2)}) collective-permute-start(bf16[2,128,768]{2,1,0:T(8,128)(2,1)S(1)} %get-tuple-element.13), channel_id=1, source_target_pairs={{0,20},{4,24},{8,28},{12,16},{16,4},{20,8},{24,12},{28,0},{1,21},{... | collective-permute-start | bytes 1179656 | tf_op jit(solution)/shard_map/ppermute | solution.py:213
  112.3 36.1 %collective-permute-start.5 = (bf16[2,128,768]{2,1,0:T(8,128)(2,1)S(1)}, bf16[2,128,768]{2,1,0:T(8,128)(2,1)S(1)}, u32[]{:S(2)}, u32[]{:S(2)}) collective-permute-start(bf16[2,128,768]{2,1,0:T(8,128)(2,1)S(1)} %get-tuple-element.13), channel_id=1, source_target_pairs={{0,24},{4,28},{8,16},{12,20},{16,8},{20,12},{24,0},{28,4},{1,25},{... | collective-permute-start | bytes 1179656 | tf_op jit(solution)/shard_map/ppermute | solution.py:213
  116.9 6.1 %copy-start.9 = (bf16[1024,768]{1,0:T(8,128)(2,1)}, bf16[1024,768]{1,0:T(8,128)(2,1)S(1)}, u32[]{:S(2)}) copy-start(bf16[1024,768]{1,0:T(8,128)(2,1)S(1)} %collective-permute-done.10.left_ref) | copy-start | bytes 4718596
  116.9 56.2 %collective-permute-start.6 = (bf16[2,128,768]{2,1,0:T(8,128)(2,1)S(1)}, bf16[2,128,768]{2,1,0:T(8,128)(2,1)S(1)}, u32[]{:S(2)}, u32[]{:S(2)}) collective-permute-start(bf16[2,128,768]{2,1,0:T(8,128)(2,1)S(1)} %get-tuple-element.13), channel_id=1, source_target_pairs={{0,28},{4,16},{8,20},{12,24},{16,12},{20,0},{24,4},{28,8},{1,29},{... | collective-permute-start | bytes 1179656 | tf_op jit(solution)/shard_map/ppermute | solution.py:213
  121.7 5.5 %copy-start.10 = (bf16[1024,768]{1,0:T(8,128)(2,1)}, bf16[1024,768]{1,0:T(8,128)(2,1)S(1)}, u32[]{:S(2)}) copy-start(bf16[1024,768]{1,0:T(8,128)(2,1)S(1)} %collective-permute-done.12.right_ref) | copy-start | bytes 4718596
  121.7 54.3 %collective-permute-start.11 = (bf16[512,768]{1,0:T(8,128)(2,1)S(1)}, bf16[512,768]{1,0:T(8,128)(2,1)S(1)}, u32[]{:S(2)}, u32[]{:S(2)}) collective-permute-start(bf16[512,768]{1,0:T(8,128)(2,1)S(1)} %slice.26), channel_id=1, source_target_pairs={{0,1},{1,2},{2,3},{3,0},{4,5},{5,6},{6,7},{7,4},{8,9},{9,10},{10,1... | collective-permute-start | bytes 2359304 | tf_op jit(solution)/shard_map/ppermute | solution.py:131
  123.1 53.8 %collective-permute-start.13 = (bf16[512,768]{1,0:T(8,128)(2,1)S(1)}, bf16[512,768]{1,0:T(8,128)(2,1)S(1)}, u32[]{:S(2)}, u32[]{:S(2)}) collective-permute-start(bf16[512,768]{1,0:T(8,128)(2,1)S(1)} %slice.27), channel_id=1, source_target_pairs={{0,3},{1,0},{2,1},{3,2},{4,7},{5,4},{6,5},{7,6},{8,11},{9,8},{10,9... | collective-permute-start | bytes 2359304 | tf_op jit(solution)/shard_map/ppermute | solution.py:131
  176.0 0.9 copy-start.2
  176.9 0.9 copy-start.5
  177.8 1.1 copy-start.3
  178.9 1.1 copy-start.6
  189.8 58.1 %collective-permute-start.14 = (bf16[768,768]{1,0:T(8,128)(2,1)}, bf16[768,768]{1,0:T(8,128)(2,1)S(1)}, u32[]{:S(2)}, u32[]{:S(2)}) collective-permute-start(bf16[768,768]{1,0:T(8,128)(2,1)} %shard_map.95), channel_id=1, source_target_pairs={{0,224},{32,192},{64,160},{96,128},{128,96},{160,64},{192,32},{224... | collective-permute-start | bytes 3538952 | tf_op jit(solution)/shard_map/ppermute | solution.py:253
  197.7 1.1 copy-start.4
  198.8 1.1 copy-start.7
Sparse Core Ops, SparseCore 0:
  36.5 70.6 all-gather.6
  108.9 88.6 all-gather.4

commit v3 on v1

--- a/solution.py
+++ b/solution.py
@@ -131,9 +131,15 @@
     return lax.ppermute(block, axis, [(i, (i + shift) % count) for i in range(count)])
 
 
-def wgrad_kernel(cols_ref, own_ref, left_ref, far_lo_ref, far_hi_ref, right_ref, out_ref, acc):
+def wgrad_kernel(pieces, offs_ref, *refs):
+    piece_refs = refs[:pieces]
+    own_ref, left_ref, far_lo_ref, far_hi_ref, right_ref = refs[pieces : pieces + 5]
+    out_ref, acc, buf = refs[pieces + 5 :]
     slot = pl.program_id(0)
     half = far_lo_ref.shape[0]
+    for k, piece_ref in enumerate(piece_refs):
+        start = pl.multiple_of(offs_ref[k], 64)
+        buf[pl.ds(start, piece_ref.shape[0]), :] = piece_ref[...]
 
     def term(cols, ctx):
         return lax.dot_general(
@@ -142,42 +148,43 @@
 
     @pl.when(slot == 0)
     def _():
-        acc[...] = term(cols_ref[...], own_ref[...])
+        acc[...] = term(buf[...], own_ref[...])
 
     @pl.when(slot == 1)
     def _():
-        acc[...] += term(cols_ref[...], left_ref[...])
+        acc[...] += term(buf[...], left_ref[...])
 
     @pl.when(slot == 2)
     def _():
-        acc[...] += term(cols_ref[:half, :], far_lo_ref[...]) + term(
-            cols_ref[half:, :], far_hi_ref[...]
-        )
+        acc[...] += term(buf[:half, :], far_lo_ref[...]) + term(buf[half:, :], far_hi_ref[...])
 
     @pl.when(slot == 3)
     def _():
-        out_ref[...] = (acc[...] + term(cols_ref[...], right_ref[...])).astype(out_ref.dtype)
-
-
-def weight_block(cols, ctx_parts):
-    slots, tokens, rows = cols.shape
-    width = ctx_parts[0].shape[1]
-    full = pl.BlockSpec((tokens, width), lambda s: (0, 0))
-    half = pl.BlockSpec((tokens // 2, width), lambda s: (0, 0))
+        out_ref[...] = (acc[...] + term(buf[...], right_ref[...])).astype(out_ref.dtype)
+
+
+def weight_block(piece_list, offsets, ctx_parts):
+    slots = piece_list[0].shape[0]
+    tokens, width = ctx_parts[0].shape
+    rows = piece_list[0].shape[2]
+    full = pl.BlockSpec((tokens, width), lambda s, o: (0, 0))
+    half = pl.BlockSpec((tokens // 2, width), lambda s, o: (0, 0))
+    piece_specs = [
+        pl.BlockSpec((None, piece.shape[1], rows), lambda s, o: (s, 0, 0)) for piece in piece_list
+    ]
     return pl.pallas_call(
-        wgrad_kernel,
+        functools.partial(wgrad_kernel, len(piece_list)),
         out_shape=jax.ShapeDtypeStruct((rows, width), jnp.bfloat16),
-        grid=(slots,),
-        in_specs=[
-            pl.BlockSpec((None, tokens, rows), lambda s: (s, 0, 0)),
-            full,
-            full,
-            half,
-            half,
-            full,
-        ],
-        out_specs=pl.BlockSpec((rows, width), lambda s: (0, 0)),
-        scratch_shapes=[pltpu.VMEM((rows, width), jnp.float32)],
+        grid_spec=pltpu.PrefetchScalarGridSpec(
+            num_scalar_prefetch=1,
+            grid=(slots,),
+            in_specs=piece_specs + [full, full, half, half, full],
+            out_specs=pl.BlockSpec((rows, width), lambda s, o: (0, 0)),
+            scratch_shapes=[
+                pltpu.VMEM((rows, width), jnp.float32),
+                pltpu.VMEM((tokens, rows), jnp.bfloat16),
+            ],
+        ),
         compiler_params=pltpu.CompilerParams(
             dimension_semantics=("arbitrary",), vmem_limit_bytes=48 * 1024 * 1024
         ),
@@ -186,7 +193,53 @@
             transcendentals=0,
             bytes_accessed=2 * slots * tokens * (rows + width) + 2 * rows * width,
         ),
-    )(cols, *ctx_parts)
+    )(offsets, *piece_list, *ctx_parts)
+
+
+def gather_over_tensor(block):
+    count = lax.axis_size("tensor")
+    along_y = 4 if count % 4 == 0 else count
+    along_z = count // along_y
+    pos = lax.axis_index("tensor")
+    zl = pos // along_y
+    y = pos % along_y
+    rows = block.shape[1]
+    split = rows // 2
+
+    def place(dz, dy):
+        return (((zl + dz) % along_z) * along_y + (y + dy) % along_y) * rows
+
+    def yshift(x, k):
+        route = [(t, (t // along_y) * along_y + (t % along_y + k) % along_y) for t in range(count)]
+        return lax.ppermute(x, "tensor", route)
+
+    def zshift(x):
+        route = [(t, ((t // along_y + 1) % along_z) * along_y + t % along_y) for t in range(count)]
+        return lax.ppermute(x, "tensor", route)
+
+    z_piece = zshift(block)
+    from_left = yshift(block, 1)
+    from_right = yshift(block, -1)
+    z_left = yshift(z_piece, 1)
+    z_right = yshift(z_piece, -1)
+    far_a = yshift(from_left[:, :split], 1)
+    far_b = yshift(from_right[:, split:], -1)
+    z_far_a = zshift(far_a)
+    z_far_b = zshift(far_b)
+    pieces = [block, z_piece, from_left, from_right, z_left, z_right, far_a, far_b, z_far_a, z_far_b]
+    offsets = [
+        place(0, 0),
+        place(1, 0),
+        place(0, -1),
+        place(0, 1),
+        place(1, -1),
+        place(1, 1),
+        place(0, 2),
+        place(0, 2) + split,
+        place(1, 2),
+        place(1, 2) + split,
+    ]
+    return pieces, jnp.stack(offsets).astype(jnp.int32)
 
 
 def on_device(queries, key_heads, value_heads, context_grad, output_grad, random_blocks):
@@ -199,16 +252,15 @@
     width_model = output_grad.shape[3]
     quarter = width_model // (2 * dp_count)
     pieces = output_grad[0, 0].reshape(rows_here, 2, dp_count, quarter).transpose(2, 1, 0, 3)
+    pieces = jnp.where(upper_half == 1, pieces, pieces[:, ::-1])
     received = [lax.dynamic_index_in_dim(pieces, dp_pos, 0, keepdims=False)]
     for shift in range(1, dp_count):
         target = (dp_pos + shift) % dp_count
         outgoing = lax.dynamic_index_in_dim(pieces, target, 0, keepdims=False)
         received.append(shift_over(outgoing, "dp", shift))
     moved = jnp.stack(received)
-    send_cols = lax.dynamic_index_in_dim(moved, 1 - upper_half, 1, keepdims=False)
-    keep_cols = lax.dynamic_index_in_dim(moved, upper_half, 1, keepdims=False)
-    send_all = lax.all_gather(send_cols, "tensor", axis=1, tiled=True)
-    keep_all = lax.all_gather(keep_cols, "tensor", axis=1, tiled=True)
+    send_pieces, offsets = gather_over_tensor(moved[:, 0])
+    keep_pieces, _ = gather_over_tensor(moved[:, 1])
 
     query_grad, key_grad, value_grad, ctx_rows = attention_backward(
         queries[0, 0], key_heads[0, 0], value_heads[0, 0], context_grad[0, 0], random_blocks
@@ -221,11 +273,11 @@
     far_hi = shift_over(from_right[split:], "dp", -1)
     ctx_parts = (ctx_rows, from_left, far_lo, far_hi, from_right)
 
-    send_block = weight_block(send_all, ctx_parts)
+    send_block = weight_block(send_pieces, offsets, ctx_parts)
     incoming = lax.ppermute(
         send_block, "pipe", [(i, pipe_count - 1 - i) for i in range(pipe_count)]
     )
-    keep_block = weight_block(keep_all, ctx_parts)
+    keep_block = weight_block(keep_pieces, offsets, ctx_parts)
     weight_grad = (keep_block.astype(jnp.float32) + incoming.astype(jnp.float32)).astype(
         jnp.bfloat16
     )[None]

time: 232 us -> 231 us (level)
  starting transfers between devices: 18.4 us -> 39.4 us
  between operations: 14.3 us -> 0.87 us
  waiting for transfers between devices: 129 us -> 119 us
  Pallas kernels: 54.3 us -> 59.7 us
  local copies, waits for them, and re-layouts: 12.6 us -> 9.04 us
    ppermute x0 -> x18, waiting for transfers between devices: none -> 87.7 us  [the longest x6 50.4 us: zshift(): return lax.ppermute(x, 'tensor', route)]
    all_gather x2 -> x0, waiting for transfers between devices: 58.5 us -> none  [the longest x1 58.5 us: on_device(): keep_all = lax.all_gather(keep_cols, 'tensor', axis=1, tiled=True)]
    ppermute x7, waiting for transfers between devices: 69.4 us -> 31.4 us  [shift_over(): lax.ppermute(block, axis, [(i, (i + shift) % count) for i in range(count)])]
    ppermute x0 -> x18, starting transfers between devices: none -> 22.9 us  [the longest x12 16 us: yshift(): return lax.ppermute(x, 'tensor', route)]
    unnamed x32, local copies, waits for them, and re-layouts: 11 us -> 5.03 us
    pallas_call x2, Pallas kernels: 16.6 us -> 22 us  [weight_block(): pl.pallas_call(functools.partial(wgrad_kernel, len(piece_list)), out_shap...]
    ppermute x7, starting transfers between devices: 10.3 us -> 7.56 us  [shift_over(): lax.ppermute(block, axis, [(i, (i + shift) % count) for i in range(count)])]
  transfers between devices with their start and end apart: 10 -> 26, of which waited for: 6 -> 12; matrix products, arithmetic and copies ran while one was open for 0% -> 1% of each run, Pallas kernels for 24% -> 26%
where the time goes in v3:
time: 231 us
  waiting for transfers between devices  119 us (52%)
  Pallas kernels  59.7 us (26%)
  starting transfers between devices  39.4 us (17%)
  local copies, waits for them, and re-layouts  9.04 us (4%)
  other arithmetic  3.03 us (1%)
    ppermute x6, waiting for transfers between devices, zshift(): return lax.ppermute(x, 'tensor', route)  50.4 us
    pallas_call x1, Pallas kernels, attention_backward(): call(rb_flat, queries, key_heads, value_heads, context_grad)  37.8 us
    ppermute x12, waiting for transfers between devices, yshift(): return lax.ppermute(x, 'tensor', route)  37.3 us
    ppermute x7, waiting for transfers between devices, shift_over(): lax.ppermute(block, axis, [(i, (i + shift) % count) for i in range(count)])  31.4 us
    pallas_call x2, Pallas kernels, weight_block(): pl.pallas_call(functools.partial(wgrad_kernel, len(piece_list)), out_shap...  22 us
    ppermute x12, starting transfers between devices, yshift(): return lax.ppermute(x, 'tensor', route)  16 us
    ppermute x1, starting transfers between devices, on_device(): lax.ppermute(send_block, 'pipe', [(i, pipe_count - 1 - i) for i in range(...  8.91 us
    ppermute x7, starting transfers between devices, shift_over(): lax.ppermute(block, axis, [(i, (i + shift) % count) for i in range(count)])  7.56 us
  transfers between devices with their start and end apart: 26, of which 12 were waited for; matrix products, arithmetic and copies ran while one was open for 1% of the time, Pallas kernels for 26%

profile of v3, /device:TPU:1, one launch (start us, length us, event | category | flops | bytes accessed | tf_op | source)
XLA Modules:
  0.0 231.1 jit_solution(14562149506424290342)
XLA Ops:
  0.7 1.9 copy.11
  3.6 1.0 constant_dynamic-slice_fusion
  4.6 3.3 %collective-permute-start.2 = (bf16[2,128,768]{2,1,0:T(8,128)(2,1)}, bf16[2,128,768]{2,1,0:T(8,128)(2,1)S(1)}, u32[]{:S(2)}, u32[]{:S(2)}) collective-permute-start(bf16[2,128,768]{2,1,0:T(8,128)(2,1)} %get-tuple-element.15), channel_id=1, source_target_pairs={{0,3},{1,0},{2,1},{3,2},{4,7},{5,4},{6,5},{7,6},{8,11},{9,8},{10,9... | collective-permute-start | bytes 1179656 | tf_op jit(solution)/shard_map/ppermute | solution.py:131
  9.3 9.7 %collective-permute-done.2 = bf16[2,128,768]{2,1,0:T(8,128)(2,1)S(1)} collective-permute-done((bf16[2,128,768]{2,1,0:T(8,128)(2,1)}, bf16[2,128,768]{2,1,0:T(8,128)(2,1)S(1)}, u32[]{:S(2)}, u32[]{:S(2)}) %collective-permute-start.2) | collective-permute-done | bytes 393248 | tf_op jit(solution)/shard_map/ppermute | solution.py:131
  19.4 9.7 %collective-permute-done = bf16[2,128,768]{2,1,0:T(8,128)(2,1)S(1)} collective-permute-done((bf16[2,128,768]{2,1,0:T(8,128)(2,1)S(1)}, bf16[2,128,768]{2,1,0:T(8,128)(2,1)S(1)}, u32[]{:S(2)}, u32[]{:S(2)}) %collective-permute-start) | collective-permute-done | bytes 393248 | tf_op jit(solution)/shard_map/ppermute | solution.py:131
  29.4 1.7 collective-permute-start.16
  31.2 1.3 collective-permute-start.17
  32.5 37.8 %shard_map.93 = (bf16[1024,768]{1,0:T(8,128)(2,1)}, bf16[1024,768]{1,0:T(8,128)(2,1)S(1)}, bf16[1024,768]{1,0:T(8,128)(2,1)}, bf16[1024,768]{1,0:T(8,128)(2,1)}) custom-call(s32[252]{0:T(256)S(1)} %reshape.20.rb_ref, bf16[1024,768]{1,0:T(8,128)(2,1)S(1)} %bitcast.34, bf16[1024,768]{1,0:T(8,128)(2,1)S(1)} %bitcast.35, bf16[1024,768]{1,0:T(8,128)(2,1)} %bitcast.41, ...), custom_call_target="tpu_custom_call" | custom-call | flops 9663676416 | bytes 11010048 | tf_op jit(solution)/shard_map/pallas_call | solution.py:123
  70.2 2.7 %collective-permute-start.14 = (bf16[1024,768]{1,0:T(8,128)(2,1)S(1)}, bf16[1024,768]{1,0:T(8,128)(2,1)S(1)}, u32[]{:S(2)}, u32[]{:S(2)}) collective-permute-start(bf16[1024,768]{1,0:T(8,128)(2,1)S(1)} %get-tuple-element.11.refs_10_), channel_id=1, source_target_pairs={{0,3},{1,0},{2,1},{3,2},{4,7},{5,4},{6,5},{7,6},{8,11},{9,8},{10,9... | collective-permute-start | bytes 4718600 | tf_op jit(solution)/shard_map/ppermute | solution.py:131
  72.9 1.5 collective-permute-start.18
  74.3 1.6 collective-permute-start.3
  76.0 14.4 %collective-permute-done.18.refs_3_ = bf16[4,128,768]{2,1,0:T(8,128)(2,1)S(1)} collective-permute-done((bf16[4,128,768]{2,1,0:T(8,128)(2,1)S(1)}, bf16[4,128,768]{2,1,0:T(8,128)(2,1)S(1)}, u32[]{:S(2)}, u32[]{:S(2)}) %collective-permute-start.18) | collective-permute-done | bytes 786464 | tf_op jit(solution)/shard_map/ppermute | solution.py:214
  90.4 2.7 %collective-permute-start.5 = (bf16[4,128,768]{2,1,0:T(8,128)(2,1)S(1)}, bf16[4,128,768]{2,1,0:T(8,128)(2,1)S(1)}, u32[]{:S(2)}, u32[]{:S(2)}) collective-permute-start(bf16[4,128,768]{2,1,0:T(8,128)(2,1)S(1)} %get-tuple-element.12.refs_0_), channel_id=1, source_target_pairs={{0,12},{4,0},{8,4},{12,8},{16,28},{20,16},{24,20},{28,24},{1,13},{... | collective-permute-start | bytes 2359304 | tf_op jit(solution)/shard_map/ppermute | solution.py:214
  93.1 0.9 copy-done.7
  94.7 11.6 %collective-permute-done.12.refs_11_ = bf16[1024,768]{1,0:T(8,128)(2,1)S(1)} collective-permute-done((bf16[1024,768]{1,0:T(8,128)(2,1)S(1)}, bf16[1024,768]{1,0:T(8,128)(2,1)S(1)}, u32[]{:S(2)}, u32[]{:S(2)}) %collective-permute-start.12) | collective-permute-done | bytes 1572896 | tf_op jit(solution)/shard_map/ppermute | solution.py:131
  106.3 1.5 collective-permute-start.20
  107.9 1.4 collective-permute-start.22
  109.2 0.9 slice.35
  111.1 9.3 %collective-permute-done.21.refs_6_ = bf16[4,64,768]{2,1,0:T(8,128)(2,1)S(1)} collective-permute-done((bf16[4,64,768]{2,1,0:T(8,128)(2,1)S(1)}, bf16[4,64,768]{2,1,0:T(8,128)(2,1)S(1)}, u32[]{:S(2)}, u32[]{:S(2)}) %collective-permute-start.21) | collective-permute-done | bytes 393248 | tf_op jit(solution)/shard_map/ppermute | solution.py:214
  120.9 13.0 %collective-permute-done.22.refs_7_ = bf16[4,64,768]{2,1,0:T(8,128)(2,1)} collective-permute-done((bf16[4,64,768]{2,1,0:T(8,128)(2,1)S(1)}, bf16[4,64,768]{2,1,0:T(8,128)(2,1)}, u32[]{:S(2)}, u32[]{:S(2)}) %collective-permute-start.22) | collective-permute-done | bytes 393248 | tf_op jit(solution)/shard_map/ppermute | solution.py:214
  133.9 2.1 collective-permute-start.23
  137.6 5.7 %collective-permute-done.23.refs_8_ = bf16[4,64,768]{2,1,0:T(8,128)(2,1)} collective-permute-done((bf16[4,64,768]{2,1,0:T(8,128)(2,1)S(1)}, bf16[4,64,768]{2,1,0:T(8,128)(2,1)}, u32[]{:S(2)}, u32[]{:S(2)}) %collective-permute-start.23) | collective-permute-done | bytes 393248 | tf_op jit(solution)/shard_map/ppermute | solution.py:218
  143.3 3.5 %collective-permute-start.9 = (bf16[4,64,768]{2,1,0:T(8,128)(2,1)S(1)}, bf16[4,64,768]{2,1,0:T(8,128)(2,1)S(1)}, u32[]{:S(2)}, u32[]{:S(2)}) collective-permute-start(bf16[4,64,768]{2,1,0:T(8,128)(2,1)S(1)} %slice.34), channel_id=1, source_target_pairs={{0,12},{4,0},{8,4},{12,8},{16,28},{20,16},{24,20},{28,24},{1,13},{... | collective-permute-start | bytes 1179656 | tf_op jit(solution)/shard_map/ppermute | solution.py:214
  146.8 4.9 %collective-permute-done.24.refs_9_ = bf16[4,64,768]{2,1,0:T(8,128)(2,1)} collective-permute-done((bf16[4,64,768]{2,1,0:T(8,128)(2,1)}, bf16[4,64,768]{2,1,0:T(8,128)(2,1)}, u32[]{:S(2)}, u32[]{:S(2)}) %collective-permute-start.24) | collective-permute-done | bytes 393248 | tf_op jit(solution)/shard_map/ppermute | solution.py:218
  152.1 3.1 %collective-permute-start.7 = (bf16[4,128,768]{2,1,0:T(8,128)(2,1)}, bf16[4,128,768]{2,1,0:T(8,128)(2,1)S(1)}, u32[]{:S(2)}, u32[]{:S(2)}) collective-permute-start(bf16[4,128,768]{2,1,0:T(8,128)(2,1)} %copy-done.7), channel_id=1, source_target_pairs={{0,12},{4,0},{8,4},{12,8},{16,28},{20,16},{24,20},{28,24},{1,13},{... | collective-permute-start | bytes 2359304 | tf_op jit(solution)/shard_map/ppermute | solution.py:214
  155.2 1.1 copy-done.10
  156.4 11.1 %shard_map.95 = bf16[768,768]{1,0:T(8,128)(2,1)} custom-call(s32[10]{0:T(128)S(1)} %stack.56.offs_ref, bf16[4,128,768]{2,1,0:T(8,128)(2,1)S(1)} %get-tuple-element.13.refs_0_, bf16[4,128,768]{2,1,0:T(8,128)(2,1)} %collective-permute-done.16.refs_1_, bf16[4,128,768]{2,1,0:T(8,128)(2,1)S(1)} %copy-done.1, bf16[4,128,768]{2,1,0:T(8,128)(2,1)S(1)} %copy-done.3, ...), custom_call_target="tpu_custom_call" | custom-call | flops 4831838208 | bytes 13762560 | tf_op jit(solution)/shard_map/pallas_call | solution.py:175
  167.5 8.9 %collective-permute-start.25 = (bf16[768,768]{1,0:T(8,128)(2,1)}, bf16[768,768]{1,0:T(8,128)(2,1)S(1)}, u32[]{:S(2)}, u32[]{:S(2)}) collective-permute-start(bf16[768,768]{1,0:T(8,128)(2,1)} %shard_map.95), channel_id=1, source_target_pairs={{0,224},{32,192},{64,160},{96,128},{128,96},{160,64},{192,32},{224... | collective-permute-start | bytes 3538952 | tf_op jit(solution)/shard_map/ppermute | solution.py:277
  177.9 34.4 %collective-permute-done.10.refs_8_ = bf16[4,64,768]{2,1,0:T(8,128)(2,1)S(1)} collective-permute-done((bf16[4,64,768]{2,1,0:T(8,128)(2,1)S(1)}, bf16[4,64,768]{2,1,0:T(8,128)(2,1)S(1)}, u32[]{:S(2)}, u32[]{:S(2)}) %collective-permute-start.10) | collective-permute-done | bytes 393248 | tf_op jit(solution)/shard_map/ppermute | solution.py:218
  212.3 5.4 %collective-permute-done.11.refs_9_ = bf16[4,64,768]{2,1,0:T(8,128)(2,1)S(1)} collective-permute-done((bf16[4,64,768]{2,1,0:T(8,128)(2,1)S(1)}, bf16[4,64,768]{2,1,0:T(8,128)(2,1)S(1)}, u32[]{:S(2)}, u32[]{:S(2)}) %collective-permute-start.11) | collective-permute-done | bytes 393248 | tf_op jit(solution)/shard_map/ppermute | solution.py:218
  217.7 10.8 %shard_map.94 = bf16[768,768]{1,0:T(8,128)(2,1)} custom-call(s32[10]{0:T(128)S(1)} %stack.56.offs_ref, bf16[4,128,768]{2,1,0:T(8,128)(2,1)S(1)} %get-tuple-element.12.refs_0_, bf16[4,128,768]{2,1,0:T(8,128)(2,1)S(1)} %copy-done.8, bf16[4,128,768]{2,1,0:T(8,128)(2,1)S(1)} %collective-permute-done.4.refs_2_, ...), custom_call_target="tpu_custom_call" | custom-call | flops 4831838208 | bytes 13762560 | tf_op jit(solution)/shard_map/pallas_call | solution.py:175
  228.6 2.6 %fusion = bf16[1,768,768]{2,1,0:T(8,128)(2,1)} fusion(bf16[768,768]{1,0:T(8,128)(2,1)S(1)} %collective-permute-done.25, bf16[768,768]{1,0:T(8,128)(2,1)} %shard_map.94), kind=kLoop, calls=%fused_computation.3 | loop fusion | flops 2359296 | bytes 3538944 | tf_op jit(solution)/shard_map/broadcast_in_dim | solution.py:281
  (69 shorter events, 8.6 us)
Async XLA Ops:
  4.6 14.4 %collective-permute-start.2 = (bf16[2,128,768]{2,1,0:T(8,128)(2,1)}, bf16[2,128,768]{2,1,0:T(8,128)(2,1)S(1)}, u32[]{:S(2)}, u32[]{:S(2)}) collective-permute-start(bf16[2,128,768]{2,1,0:T(8,128)(2,1)} %get-tuple-element.15), channel_id=1, source_target_pairs={{0,3},{1,0},{2,1},{3,2},{4,7},{5,4},{6,5},{7,6},{8,11},{9,8},{10,9... | collective-permute-start | bytes 1179656 | tf_op jit(solution)/shard_map/ppermute | solution.py:131
  7.9 11.5 %collective-permute-start.1 = (bf16[2,128,768]{2,1,0:T(8,128)(2,1)}, bf16[2,128,768]{2,1,0:T(8,128)(2,1)S(1)}, u32[]{:S(2)}, u32[]{:S(2)}) collective-permute-start(bf16[2,128,768]{2,1,0:T(8,128)(2,1)} %get-tuple-element.16), channel_id=1, source_target_pairs={{0,2},{1,3},{2,0},{3,1},{4,6},{5,7},{6,4},{7,5},{8,10},{9,11},{10,... | collective-permute-start | bytes 1179656 | tf_op jit(solution)/shard_map/ppermute | solution.py:131
  8.4 20.7 %collective-permute-start = (bf16[2,128,768]{2,1,0:T(8,128)(2,1)S(1)}, bf16[2,128,768]{2,1,0:T(8,128)(2,1)S(1)}, u32[]{:S(2)}, u32[]{:S(2)}) collective-permute-start(bf16[2,128,768]{2,1,0:T(8,128)(2,1)S(1)} %get-tuple-element.17), channel_id=1, source_target_pairs={{0,1},{1,2},{2,3},{3,0},{4,5},{5,6},{6,7},{7,4},{8,9},{9,10},{10,1... | collective-permute-start | bytes 1179656 | tf_op jit(solution)/shard_map/ppermute | solution.py:131
  29.4 44.9 %collective-permute-start.16 = (bf16[4,128,768]{2,1,0:T(8,128)(2,1)S(1)}, bf16[4,128,768]{2,1,0:T(8,128)(2,1)}, u32[]{:S(2)}, u32[]{:S(2)}) collective-permute-start(bf16[4,128,768]{2,1,0:T(8,128)(2,1)S(1)} %get-tuple-element.13.refs_0_), channel_id=1, source_target_pairs={{0,16},{4,20},{8,24},{12,28},{16,0},{20,4},{24,8},{28,12},{1,17},{... | collective-permute-start | bytes 2359304 | tf_op jit(solution)/shard_map/ppermute | solution.py:218
  31.2 44.8 %collective-permute-start.17 = (bf16[4,128,768]{2,1,0:T(8,128)(2,1)S(1)}, bf16[4,128,768]{2,1,0:T(8,128)(2,1)S(1)}, u32[]{:S(2)}, u32[]{:S(2)}) collective-permute-start(bf16[4,128,768]{2,1,0:T(8,128)(2,1)S(1)} %get-tuple-element.13.refs_0_), channel_id=1, source_target_pairs={{0,4},{4,8},{8,12},{12,0},{16,20},{20,24},{24,28},{28,16},{1,5},{5... | collective-permute-start | bytes 2359304 | tf_op jit(solution)/shard_map/ppermute | solution.py:214
  70.2 40.0 %copy-start.6 = (bf16[1024,768]{1,0:T(8,128)(2,1)}, bf16[1024,768]{1,0:T(8,128)(2,1)S(1)}, u32[]{:S(2)}) copy-start(bf16[1024,768]{1,0:T(8,128)(2,1)S(1)} %get-tuple-element.11.refs_10_) | copy-start | bytes 4718596
  70.2 36.1 %collective-permute-start.12 = (bf16[1024,768]{1,0:T(8,128)(2,1)S(1)}, bf16[1024,768]{1,0:T(8,128)(2,1)S(1)}, u32[]{:S(2)}, u32[]{:S(2)}) collective-permute-start(bf16[1024,768]{1,0:T(8,128)(2,1)S(1)} %get-tuple-element.11.refs_10_), channel_id=1, source_target_pairs={{0,1},{1,2},{2,3},{3,0},{4,5},{5,6},{6,7},{7,4},{8,9},{9,10},{10,1... | collective-permute-start | bytes 4718600 | tf_op jit(solution)/shard_map/ppermute | solution.py:131
  70.2 37.6 %collective-permute-start.14 = (bf16[1024,768]{1,0:T(8,128)(2,1)S(1)}, bf16[1024,768]{1,0:T(8,128)(2,1)S(1)}, u32[]{:S(2)}, u32[]{:S(2)}) collective-permute-start(bf16[1024,768]{1,0:T(8,128)(2,1)S(1)} %get-tuple-element.11.refs_10_), channel_id=1, source_target_pairs={{0,3},{1,0},{2,1},{3,2},{4,7},{5,4},{6,5},{7,6},{8,11},{9,8},{10,9... | collective-permute-start | bytes 4718600 | tf_op jit(solution)/shard_map/ppermute | solution.py:131
  72.9 17.5 %collective-permute-start.18 = (bf16[4,128,768]{2,1,0:T(8,128)(2,1)S(1)}, bf16[4,128,768]{2,1,0:T(8,128)(2,1)S(1)}, u32[]{:S(2)}, u32[]{:S(2)}) collective-permute-start(bf16[4,128,768]{2,1,0:T(8,128)(2,1)S(1)} %get-tuple-element.13.refs_0_), channel_id=1, source_target_pairs={{0,12},{4,0},{8,4},{12,8},{16,28},{20,16},{24,20},{28,24},{1,13},{... | collective-permute-start | bytes 2359304 | tf_op jit(solution)/shard_map/ppermute | solution.py:214
  74.3 18.8 %collective-permute-start.3 = (bf16[4,128,768]{2,1,0:T(8,128)(2,1)S(1)}, bf16[4,128,768]{2,1,0:T(8,128)(2,1)S(1)}, u32[]{:S(2)}, u32[]{:S(2)}) collective-permute-start(bf16[4,128,768]{2,1,0:T(8,128)(2,1)S(1)} %get-tuple-element.12.refs_0_), channel_id=1, source_target_pairs={{0,16},{4,20},{8,24},{12,28},{16,0},{20,4},{24,8},{28,12},{1,17},{... | collective-permute-start | bytes 2359304 | tf_op jit(solution)/shard_map/ppermute | solution.py:218
  76.0 34.2 %copy-start = (bf16[4,128,768]{2,1,0:T(8,128)(2,1)}, bf16[4,128,768]{2,1,0:T(8,128)(2,1)S(1)}, u32[]{:S(2)}) copy-start(bf16[4,128,768]{2,1,0:T(8,128)(2,1)S(1)} %collective-permute-done.17.refs_2_) | copy-start | bytes 2359300
  76.0 18.7 %collective-permute-start.4 = (bf16[4,128,768]{2,1,0:T(8,128)(2,1)S(1)}, bf16[4,128,768]{2,1,0:T(8,128)(2,1)S(1)}, u32[]{:S(2)}, u32[]{:S(2)}) collective-permute-start(bf16[4,128,768]{2,1,0:T(8,128)(2,1)S(1)} %get-tuple-element.12.refs_0_), channel_id=1, source_target_pairs={{0,4},{4,8},{8,12},{12,0},{16,20},{20,24},{24,28},{28,16},{1,5},{5... | collective-permute-start | bytes 2359304 | tf_op jit(solution)/shard_map/ppermute | solution.py:214
  90.4 19.8 %copy-start.2 = (bf16[4,128,768]{2,1,0:T(8,128)(2,1)}, bf16[4,128,768]{2,1,0:T(8,128)(2,1)S(1)}, u32[]{:S(2)}) copy-start(bf16[4,128,768]{2,1,0:T(8,128)(2,1)S(1)} %collective-permute-done.18.refs_3_) | copy-start | bytes 2359300
  90.4 20.7 %collective-permute-start.5 = (bf16[4,128,768]{2,1,0:T(8,128)(2,1)S(1)}, bf16[4,128,768]{2,1,0:T(8,128)(2,1)S(1)}, u32[]{:S(2)}, u32[]{:S(2)}) collective-permute-start(bf16[4,128,768]{2,1,0:T(8,128)(2,1)S(1)} %get-tuple-element.12.refs_0_), channel_id=1, source_target_pairs={{0,12},{4,0},{8,4},{12,8},{16,28},{20,16},{24,20},{28,24},{1,13},{... | collective-permute-start | bytes 2359304 | tf_op jit(solution)/shard_map/ppermute | solution.py:214
  94.0 41.9 %collective-permute-start.19 = (bf16[4,128,768]{2,1,0:T(8,128)(2,1)}, bf16[4,128,768]{2,1,0:T(8,128)(2,1)S(1)}, u32[]{:S(2)}, u32[]{:S(2)}) collective-permute-start(bf16[4,128,768]{2,1,0:T(8,128)(2,1)} %collective-permute-done.16.refs_1_), channel_id=1, source_target_pairs={{0,4},{4,8},{8,12},{12,0},{16,20},{20,24},{24,28},{28,16},{1,5},{5... | collective-permute-start | bytes 2359304 | tf_op jit(solution)/shard_map/ppermute | solution.py:214
  94.7 25.7 %collective-permute-start.21 = (bf16[4,64,768]{2,1,0:T(8,128)(2,1)S(1)}, bf16[4,64,768]{2,1,0:T(8,128)(2,1)S(1)}, u32[]{:S(2)}, u32[]{:S(2)}) collective-permute-start(bf16[4,64,768]{2,1,0:T(8,128)(2,1)S(1)} %slice.38), channel_id=1, source_target_pairs={{0,4},{4,8},{8,12},{12,0},{16,20},{20,24},{24,28},{28,16},{1,5},{5... | collective-permute-start | bytes 1179656 | tf_op jit(solution)/shard_map/ppermute | solution.py:214
  106.3 30.7 %collective-permute-start.20 = (bf16[4,128,768]{2,1,0:T(8,128)(2,1)}, bf16[4,128,768]{2,1,0:T(8,128)(2,1)}, u32[]{:S(2)}, u32[]{:S(2)}) collective-permute-start(bf16[4,128,768]{2,1,0:T(8,128)(2,1)} %collective-permute-done.16.refs_1_), channel_id=1, source_target_pairs={{0,12},{4,0},{8,4},{12,8},{16,28},{20,16},{24,20},{28,24},{1,13},{... | collective-permute-start | bytes 2359304 | tf_op jit(solution)/shard_map/ppermute | solution.py:214
  107.9 28.1 %copy-start.12 = (bf16[1024,768]{1,0:T(8,128)(2,1)}, bf16[1024,768]{1,0:T(8,128)(2,1)S(1)}, u32[]{:S(2)}) copy-start(bf16[1024,768]{1,0:T(8,128)(2,1)S(1)} %collective-permute-done.14.refs_14_) | copy-start | bytes 4718596
  107.9 26.0 %collective-permute-start.22 = (bf16[4,64,768]{2,1,0:T(8,128)(2,1)S(1)}, bf16[4,64,768]{2,1,0:T(8,128)(2,1)}, u32[]{:S(2)}, u32[]{:S(2)}) collective-permute-start(bf16[4,64,768]{2,1,0:T(8,128)(2,1)S(1)} %slice.39), channel_id=1, source_target_pairs={{0,12},{4,0},{8,4},{12,8},{16,28},{20,16},{24,20},{28,24},{1,13},{... | collective-permute-start | bytes 1179656 | tf_op jit(solution)/shard_map/ppermute | solution.py:214
  111.1 41.0 %collective-permute-start.13 = (bf16[512,768]{1,0:T(8,128)(2,1)}, bf16[512,768]{1,0:T(8,128)(2,1)}, u32[]{:S(2)}, u32[]{:S(2)}) collective-permute-start(bf16[512,768]{1,0:T(8,128)(2,1)} %slice.35), channel_id=1, source_target_pairs={{0,1},{1,2},{2,3},{3,0},{4,5},{5,6},{6,7},{7,4},{8,9},{9,10},{10,1... | collective-permute-start | bytes 2359304 | tf_op jit(solution)/shard_map/ppermute | solution.py:131
  120.4 34.8 %collective-permute-start.15 = (bf16[512,768]{1,0:T(8,128)(2,1)}, bf16[512,768]{1,0:T(8,128)(2,1)}, u32[]{:S(2)}, u32[]{:S(2)}) collective-permute-start(bf16[512,768]{1,0:T(8,128)(2,1)} %slice.36), channel_id=1, source_target_pairs={{0,3},{1,0},{2,1},{3,2},{4,7},{5,4},{6,5},{7,6},{8,11},{9,8},{10,9... | collective-permute-start | bytes 2359304 | tf_op jit(solution)/shard_map/ppermute | solution.py:131
  133.9 9.4 %collective-permute-start.23 = (bf16[4,64,768]{2,1,0:T(8,128)(2,1)S(1)}, bf16[4,64,768]{2,1,0:T(8,128)(2,1)}, u32[]{:S(2)}, u32[]{:S(2)}) collective-permute-start(bf16[4,64,768]{2,1,0:T(8,128)(2,1)S(1)} %collective-permute-done.21.refs_6_), channel_id=1, source_target_pairs={{0,16},{4,20},{8,24},{12,28},{16,0},{20,4},{24,8},{28,12},{1,17},{... | collective-permute-start | bytes 1179656 | tf_op jit(solution)/shard_map/ppermute | solution.py:218
  136.9 14.8 %collective-permute-start.24 = (bf16[4,64,768]{2,1,0:T(8,128)(2,1)}, bf16[4,64,768]{2,1,0:T(8,128)(2,1)}, u32[]{:S(2)}, u32[]{:S(2)}) collective-permute-start(bf16[4,64,768]{2,1,0:T(8,128)(2,1)} %collective-permute-done.22.refs_7_), channel_id=1, source_target_pairs={{0,16},{4,20},{8,24},{12,28},{16,0},{20,4},{24,8},{28,12},{1,17},{... | collective-permute-start | bytes 1179656 | tf_op jit(solution)/shard_map/ppermute | solution.py:218
  137.0 80.7 %copy-start.8 = (bf16[4,128,768]{2,1,0:T(8,128)(2,1)S(1)}, bf16[4,128,768]{2,1,0:T(8,128)(2,1)}, u32[]{:S(2)}) copy-start(bf16[4,128,768]{2,1,0:T(8,128)(2,1)} %copy-done.7) | copy-start | bytes 2359300
  137.1 39.3 %collective-permute-start.8 = (bf16[4,64,768]{2,1,0:T(8,128)(2,1)S(1)}, bf16[4,64,768]{2,1,0:T(8,128)(2,1)S(1)}, u32[]{:S(2)}, u32[]{:S(2)}) collective-permute-start(bf16[4,64,768]{2,1,0:T(8,128)(2,1)S(1)} %slice.33), channel_id=1, source_target_pairs={{0,4},{4,8},{8,12},{12,0},{16,20},{20,24},{24,28},{28,16},{1,5},{5... | collective-permute-start | bytes 1179656 | tf_op jit(solution)/shard_map/ppermute | solution.py:214
  143.3 33.9 %collective-permute-start.9 = (bf16[4,64,768]{2,1,0:T(8,128)(2,1)S(1)}, bf16[4,64,768]{2,1,0:T(8,128)(2,1)S(1)}, u32[]{:S(2)}, u32[]{:S(2)}) collective-permute-start(bf16[4,64,768]{2,1,0:T(8,128)(2,1)S(1)} %slice.34), channel_id=1, source_target_pairs={{0,12},{4,0},{8,4},{12,8},{16,28},{20,16},{24,20},{28,24},{1,13},{... | collective-permute-start | bytes 1179656 | tf_op jit(solution)/shard_map/ppermute | solution.py:214
  151.7 26.2 %collective-permute-start.6 = (bf16[4,128,768]{2,1,0:T(8,128)(2,1)}, bf16[4,128,768]{2,1,0:T(8,128)(2,1)S(1)}, u32[]{:S(2)}, u32[]{:S(2)}) collective-permute-start(bf16[4,128,768]{2,1,0:T(8,128)(2,1)} %copy-done.7), channel_id=1, source_target_pairs={{0,4},{4,8},{8,12},{12,0},{16,20},{20,24},{24,28},{28,16},{1,5},{5... | collective-permute-start | bytes 2359304 | tf_op jit(solution)/shard_map/ppermute | solution.py:214
  152.1 25.8 %collective-permute-start.7 = (bf16[4,128,768]{2,1,0:T(8,128)(2,1)}, bf16[4,128,768]{2,1,0:T(8,128)(2,1)S(1)}, u32[]{:S(2)}, u32[]{:S(2)}) collective-permute-start(bf16[4,128,768]{2,1,0:T(8,128)(2,1)} %copy-done.7), channel_id=1, source_target_pairs={{0,12},{4,0},{8,4},{12,8},{16,28},{20,16},{24,20},{28,24},{1,13},{... | collective-permute-start | bytes 2359304 | tf_op jit(solution)/shard_map/ppermute | solution.py:214
  167.5 61.1 %collective-permute-start.25 = (bf16[768,768]{1,0:T(8,128)(2,1)}, bf16[768,768]{1,0:T(8,128)(2,1)S(1)}, u32[]{:S(2)}, u32[]{:S(2)}) collective-permute-start(bf16[768,768]{1,0:T(8,128)(2,1)} %shard_map.95), channel_id=1, source_target_pairs={{0,224},{32,192},{64,160},{96,128},{128,96},{160,64},{192,32},{224... | collective-permute-start | bytes 3538952 | tf_op jit(solution)/shard_map/ppermute | solution.py:277
  176.4 35.9 %collective-permute-start.10 = (bf16[4,64,768]{2,1,0:T(8,128)(2,1)S(1)}, bf16[4,64,768]{2,1,0:T(8,128)(2,1)S(1)}, u32[]{:S(2)}, u32[]{:S(2)}) collective-permute-start(bf16[4,64,768]{2,1,0:T(8,128)(2,1)S(1)} %collective-permute-done.8.refs_6_), channel_id=1, source_target_pairs={{0,16},{4,20},{8,24},{12,28},{16,0},{20,4},{24,8},{28,12},{1,17},{... | collective-permute-start | bytes 1179656 | tf_op jit(solution)/shard_map/ppermute | solution.py:218
  177.1 40.6 %collective-permute-start.11 = (bf16[4,64,768]{2,1,0:T(8,128)(2,1)S(1)}, bf16[4,64,768]{2,1,0:T(8,128)(2,1)S(1)}, u32[]{:S(2)}, u32[]{:S(2)}) collective-permute-start(bf16[4,64,768]{2,1,0:T(8,128)(2,1)S(1)} %collective-permute-done.9.refs_7_), channel_id=1, source_target_pairs={{0,16},{4,20},{8,24},{12,28},{16,0},{20,4},{24,8},{28,12},{1,17},{... | collective-permute-start | bytes 1179656 | tf_op jit(solution)/shard_map/ppermute | solution.py:218
  177.9 39.8 %copy-start.14 = (bf16[4,128,768]{2,1,0:T(8,128)(2,1)}, bf16[4,128,768]{2,1,0:T(8,128)(2,1)S(1)}, u32[]{:S(2)}) copy-start(bf16[4,128,768]{2,1,0:T(8,128)(2,1)S(1)} %collective-permute-done.7.refs_5_) | copy-start | bytes 2359300
  (9 other events, 56.0 us)

commit v4 on v3

--- a/solution.py
+++ b/solution.py
@@ -12,11 +12,11 @@
 ROWS = 256
 
 
-def attention_kernel(
-    blocks, head_size, rb_ref, q_ref, k_ref, v_ref, g_ref, dq_ref, ctx_ref, dk_ref, dv_ref,
-    dk_acc, dv_acc,
-):
-    head = pl.program_id(0)
+def attention_kernel(blocks, head_size, head0, aliased, rb_ref, q_ref, k_ref, v_ref, g_ref, *rest):
+    if aliased:
+        rest = rest[4:]
+    dq_ref, ctx_ref, dk_ref, dv_ref, dk_acc, dv_acc = rest
+    head = pl.program_id(0) + head0
     chunk = pl.program_id(1)
     score_scale = 1.0 / math.sqrt(head_size)
     tokens = k_ref.shape[0]
@@ -86,44 +86,46 @@
         dv_ref[...] = dv_acc[...].astype(jnp.bfloat16)
 
 
-def attention_backward(queries, key_heads, value_heads, context_grad, random_blocks):
+def attention_call(index, queries, key_heads, value_heads, context_grad, random_blocks, results):
     heads_here = random_blocks.shape[0]
     tokens, width_here = queries.shape
     head_size = width_here // heads_here
     blocks = tokens // BLK
     chunks = tokens // ROWS
+    group = 2 if heads_here % 2 == 0 else 1
+    head0 = index * group
     rb_flat = random_blocks.reshape(-1)
-    row_spec = pl.BlockSpec((ROWS, head_size), lambda h, c, rb: (c, h))
-    full_spec = pl.BlockSpec((tokens, head_size), lambda h, c, rb: (0, h))
     out_shape = jax.ShapeDtypeStruct((tokens, width_here), jnp.bfloat16)
-    flops = 2 * tokens * tokens * head_size * 6 * heads_here
+    row_spec = pl.BlockSpec((ROWS, head_size), lambda h, c, rb: (c, h + head0))
+    full_spec = pl.BlockSpec((tokens, head_size), lambda h, c, rb: (0, h + head0))
+    aliased = results is not None
+    extra = [pl.BlockSpec(memory_space=pl.ANY)] * 4 if aliased else []
     call = pl.pallas_call(
-        functools.partial(attention_kernel, blocks, head_size),
+        functools.partial(attention_kernel, blocks, head_size, head0, aliased),
         out_shape=(out_shape, out_shape, out_shape, out_shape),
         grid_spec=pltpu.PrefetchScalarGridSpec(
             num_scalar_prefetch=1,
-            grid=(heads_here, chunks),
-            in_specs=[row_spec, full_spec, full_spec, row_spec],
+            grid=(group, chunks),
+            in_specs=[row_spec, full_spec, full_spec, row_spec] + extra,
             out_specs=[row_spec, row_spec, full_spec, full_spec],
             scratch_shapes=[
                 pltpu.VMEM((tokens, head_size), jnp.float32),
                 pltpu.VMEM((tokens, head_size), jnp.float32),
             ],
         ),
+        input_output_aliases={5: 0, 6: 1, 7: 2, 8: 3} if aliased else {},
         compiler_params=pltpu.CompilerParams(
             dimension_semantics=("arbitrary", "arbitrary"),
             vmem_limit_bytes=48 * 1024 * 1024,
         ),
         cost_estimate=pl.CostEstimate(
-            flops=flops,
-            transcendentals=tokens * tokens * heads_here,
-            bytes_accessed=7 * tokens * width_here * 2,
-        ),
-    )
-    query_grad, context, key_grad, value_grad = call(
-        rb_flat, queries, key_heads, value_heads, context_grad
-    )
-    return query_grad, key_grad, value_grad, context
+            flops=2 * tokens * tokens * head_size * 6 * group,
+            transcendentals=tokens * tokens * group,
+            bytes_accessed=7 * tokens * head_size * group * 2,
+        ),
+    )
+    args = (rb_flat, queries, key_heads, value_heads, context_grad)
+    return call(*args, *results) if aliased else call(*args)
 
 
 def shift_over(block, axis, shift):
@@ -196,10 +198,27 @@
     )(offsets, *piece_list, *ctx_parts)
 
 
-def gather_over_tensor(block):
+def tensor_layout():
     count = lax.axis_size("tensor")
     along_y = 4 if count % 4 == 0 else count
     along_z = count // along_y
+    return count, along_y, along_z
+
+
+def yshift(x, k):
+    count, along_y, _ = tensor_layout()
+    route = [(t, (t // along_y) * along_y + (t % along_y + k) % along_y) for t in range(count)]
+    return lax.ppermute(x, "tensor", route)
+
+
+def zshift(x):
+    count, along_y, along_z = tensor_layout()
+    route = [(t, ((t // along_y + 1) % along_z) * along_y + t % along_y) for t in range(count)]
+    return lax.ppermute(x, "tensor", route)
+
+
+def gather_steps(block, last_over_z, between=lambda step, values: values):
+    count, along_y, along_z = tensor_layout()
     pos = lax.axis_index("tensor")
     zl = pos // along_y
     y = pos % along_y
@@ -209,24 +228,21 @@
     def place(dz, dy):
         return (((zl + dz) % along_z) * along_y + (y + dy) % along_y) * rows
 
-    def yshift(x, k):
-        route = [(t, (t // along_y) * along_y + (t % along_y + k) % along_y) for t in range(count)]
-        return lax.ppermute(x, "tensor", route)
-
-    def zshift(x):
-        route = [(t, ((t // along_y + 1) % along_z) * along_y + t % along_y) for t in range(count)]
-        return lax.ppermute(x, "tensor", route)
-
-    z_piece = zshift(block)
-    from_left = yshift(block, 1)
-    from_right = yshift(block, -1)
-    z_left = yshift(z_piece, 1)
-    z_right = yshift(z_piece, -1)
-    far_a = yshift(from_left[:, :split], 1)
-    far_b = yshift(from_right[:, split:], -1)
-    z_far_a = zshift(far_a)
-    z_far_b = zshift(far_b)
-    pieces = [block, z_piece, from_left, from_right, z_left, z_right, far_a, far_b, z_far_a, z_far_b]
+    source = between(0, block)
+    first = (zshift(source), yshift(source, 1), yshift(source, -1))
+    z_piece, from_left, from_right = between(1, first)
+    second = (
+        yshift(z_piece, 1),
+        yshift(z_piece, -1),
+        yshift(from_left[:, :split], 1),
+        yshift(from_right[:, split:], -1),
+    )
+    z_left, z_right, far_a, far_b = between(2, second)
+    if last_over_z:
+        third = (zshift(far_a), zshift(far_b))
+    else:
+        third = (yshift(z_left[:, :split], 1), yshift(z_right[:, split:], -1))
+    pieces = [block, *first, *second, *third]
     offsets = [
         place(0, 0),
         place(1, 0),
@@ -259,12 +275,23 @@
         outgoing = lax.dynamic_index_in_dim(pieces, target, 0, keepdims=False)
         received.append(shift_over(outgoing, "dp", shift))
     moved = jnp.stack(received)
-    send_pieces, offsets = gather_over_tensor(moved[:, 0])
-    keep_pieces, _ = gather_over_tensor(moved[:, 1])
-
-    query_grad, key_grad, value_grad, ctx_rows = attention_backward(
-        queries[0, 0], key_heads[0, 0], value_heads[0, 0], context_grad[0, 0], random_blocks
-    )
+    attn_in = (queries[0, 0], key_heads[0, 0], value_heads[0, 0], context_grad[0, 0])
+    calls = 3 if random_blocks.shape[0] % 6 == 0 else random_blocks.shape[0]
+    state = {"results": None}
+
+    def between(step, values):
+        if step < calls:
+            state["results"] = attention_call(
+                step, *attn_in, random_blocks, state["results"]
+            )
+        values, _ = lax.optimization_barrier((values, state["results"][1]))
+        return values
+
+    send_pieces, offsets = gather_steps(moved[:, 0], True, between)
+    for index in range(3, calls):
+        state["results"] = attention_call(index, *attn_in, random_blocks, state["results"])
+    keep_pieces, _ = gather_steps(moved[:, 1], False)
+    query_grad, ctx_rows, key_grad, value_grad = state["results"]
     tokens_all = ctx_rows.shape[0]
     split = tokens_all // 2
     from_left = shift_over(ctx_rows, "dp", 1)

time: 231 us -> 217 us (0.939)
  waiting for transfers between devices: 119 us -> 88.1 us
  local copies, waits for them, and re-layouts: 9.04 us -> 14.9 us
  Pallas kernels: 59.7 us -> 64.7 us
  other arithmetic: 3.03 us -> 5.41 us
    ppermute x6 -> x4, waiting for transfers between devices: 50.4 us -> 24.2 us  [zshift(): return lax.ppermute(x, 'tensor', route)]
    ppermute x12 -> x14, waiting for transfers between devices: 37.3 us -> 19.5 us  [yshift(): return lax.ppermute(x, 'tensor', route)]
    ppermute x1, waiting for transfers between devices: 0.01 us -> 16.8 us  [on_device(): lax.ppermute(send_block, 'pipe', [(i, pipe_count - 1 - i) for i in range(...]
    pallas_call x1 -> x3, Pallas kernels: 37.8 us -> 42.3 us  [attention_call(): return call(*args, *results) if aliased else call(*args)]
    ppermute x7, waiting for transfers between devices: 31.4 us -> 27.7 us  [shift_over(): lax.ppermute(block, axis, [(i, (i + shift) % count) for i in range(count)])]
    slice x4 -> x6, local copies, waits for them, and re-layouts: 0.11 us -> 3.16 us  [the longest x2 2.05 us: gather_steps(): third = (yshift(z_left[:, :split], 1), yshift(z_right[:, split:], -1))]
    ppermute x6 -> x4, starting transfers between devices: 6.95 us -> 4.06 us  [zshift(): return lax.ppermute(x, 'tensor', route)]
    ppermute x12 -> x14, starting transfers between devices: 16 us -> 18.3 us  [yshift(): return lax.ppermute(x, 'tensor', route)]
  transfers between devices with their start and end apart: 26 -> 26, of which waited for: 12 -> 13; matrix products, arithmetic and copies ran while one was open for 1% -> 3% of each run, Pallas kernels for 26% -> 24%
where the time goes in v4:
time: 217 us; the launch traced here: 215 us
  waiting for transfers between devices  88.1 us (41%)
  Pallas kernels  64.7 us (30%)
  starting transfers between devices  41 us (19%)
  local copies, waits for them, and re-layouts  14.9 us (7%)
  other arithmetic  5.41 us (2%)
    pallas_call x3, Pallas kernels, attention_call(): return call(*args, *results) if aliased else call(*args)  42.3 us
    ppermute x7, waiting for transfers between devices, shift_over(): lax.ppermute(block, axis, [(i, (i + shift) % count) for i in range(count)])  27.7 us
    ppermute x4, waiting for transfers between devices, zshift(): return lax.ppermute(x, 'tensor', route)  24.2 us
    pallas_call x2, Pallas kernels, weight_block(): pl.pallas_call(functools.partial(wgrad_kernel, len(piece_list)), out_shap...  22.3 us
    ppermute x14, waiting for transfers between devices, yshift(): return lax.ppermute(x, 'tensor', route)  19.5 us
    ppermute x14, starting transfers between devices, yshift(): return lax.ppermute(x, 'tensor', route)  18.3 us
    ppermute x1, waiting for transfers between devices, on_device(): lax.ppermute(send_block, 'pipe', [(i, pipe_count - 1 - i) for i in range(...  16.8 us
    ppermute x7, starting transfers between devices, shift_over(): lax.ppermute(block, axis, [(i, (i + shift) % count) for i in range(count)])  9.84 us
  transfers between devices with their start and end apart: 26, of which 13 were waited for; matrix products, arithmetic and copies ran while one was open for 3% of the time, Pallas kernels for 24%

profile of v4, /device:TPU:1, one launch (start us, length us, event | category | flops | bytes accessed | tf_op | source)
XLA Modules:
  0.0 215.1 jit_solution(7774424589321979481)
XLA Ops:
  0.7 1.9 copy.19
  3.3 1.4 reverse_select_fusion
  4.7 2.7 %constant_dynamic-slice_fusion = (bf16[1,2,128,768]{3,2,0,1:T(8,128)(2,1)}, bf16[2,128,768]{2,1,0:T(8,128)(2,1)}, bf16[2,128,768]{2,1,0:T(8,128)(2,1)}, bf16[2,128,768]{2,1,0:T(8,128)(2,1)}) fusion(bf16[4,2,128,768]{3,2,0,1:T(8,128)(2,1)} %reverse_select_fusion, s32[]{:T(128)S(6)} %select_n.106, s32[]{:T(128)S(6)} %select_n.112, s32[]{:T(128)S(6)} %select_n.110, ...), kind=kLoop, calls=%fused_computation.9 | loop fusion | bytes 3145744 | tf_op jit(solution)/shard_map/jit(dynamic_index_in_dim)/dynamic_slice | solution.py:272
  7.4 3.3 %collective-permute-start.2 = (bf16[2,128,768]{2,1,0:T(8,128)(2,1)}, bf16[2,128,768]{2,1,0:T(8,128)(2,1)}, u32[]{:S(2)}, u32[]{:S(2)}) collective-permute-start(bf16[2,128,768]{2,1,0:T(8,128)(2,1)} %get-tuple-element.43), channel_id=1, source_target_pairs={{0,3},{1,0},{2,1},{3,2},{4,7},{5,4},{6,5},{7,6},{8,11},{9,8},{10,9... | collective-permute-start | bytes 1179656 | tf_op jit(solution)/shard_map/ppermute | solution.py:133
  12.1 14.1 %shard_map.93 = (bf16[1024,768]{1,0:T(8,128)(2,1)}, bf16[1024,768]{1,0:T(8,128)(2,1)S(1)}, bf16[1024,768]{1,0:T(8,128)(2,1)}, bf16[1024,768]{1,0:T(8,128)(2,1)}) custom-call(s32[252]{0:T(256)S(1)} %reshape.22.rb_ref, bf16[1024,768]{1,0:T(8,128)(2,1)S(1)} %bitcast.34, bf16[1024,768]{1,0:T(8,128)(2,1)S(1)} %bitcast.37, bf16[1024,768]{1,0:T(8,128)(2,1)} %bitcast.40, ...), custom_call_target="tpu_custom_call" | custom-call | flops 3221225472 | bytes 3670016 | tf_op jit(solution)/shard_map/pallas_call | solution.py:128
  26.3 5.7 %collective-permute-done = bf16[2,128,768]{2,1,0:T(8,128)(2,1)} collective-permute-done((bf16[2,128,768]{2,1,0:T(8,128)(2,1)}, bf16[2,128,768]{2,1,0:T(8,128)(2,1)}, u32[]{:S(2)}, u32[]{:S(2)}) %collective-permute-start) | collective-permute-done | bytes 393248 | tf_op jit(solution)/shard_map/ppermute | solution.py:133
  32.0 1.4 pad_maximum_fusion
  34.4 1.6 collective-permute-start.16
  37.4 1.4 collective-permute-start.18
  38.8 14.1 %shard_map.94 = (bf16[1024,768]{1,0:T(8,128)(2,1)}, bf16[1024,768]{1,0:T(8,128)(2,1)S(1)}, bf16[1024,768]{1,0:T(8,128)(2,1)}, bf16[1024,768]{1,0:T(8,128)(2,1)}) custom-call(s32[252]{0:T(256)S(1)} %reshape.22.rb_ref, bf16[1024,768]{1,0:T(8,128)(2,1)S(1)} %bitcast.35, ...), custom_call_target="tpu_custom_call", output_to_operand_aliasing={{0}: (5, {}), {1}: (6, {}), {2}: (7, {}), {3}: (8, {})} | custom-call | flops 3221225472 | bytes 3670016 | tf_op jit(solution)/shard_map/pallas_call | solution.py:128
  53.4 2.3 %collective-permute-done.17.refs_2_ = bf16[4,128,768]{2,1,0:T(8,128)(2,1)S(1)} collective-permute-done((bf16[4,128,768]{2,1,0:T(8,128)(2,1)S(1)}, bf16[4,128,768]{2,1,0:T(8,128)(2,1)S(1)}, u32[]{:S(2)}, u32[]{:S(2)}) %collective-permute-start.17) | collective-permute-done | bytes 786464 | tf_op jit(solution)/shard_map/ppermute | solution.py:211
  55.7 14.1 %shard_map.95 = (bf16[1024,768]{1,0:T(8,128)(2,1)}, bf16[1024,768]{1,0:T(8,128)(2,1)S(1)}, bf16[1024,768]{1,0:T(8,128)(2,1)}, bf16[1024,768]{1,0:T(8,128)(2,1)}) custom-call(s32[252]{0:T(256)S(1)} %reshape.22.rb_ref, bf16[1024,768]{1,0:T(8,128)(2,1)S(1)} %bitcast.36, ...), custom_call_target="tpu_custom_call", output_to_operand_aliasing={{0}: (5, {}), {1}: (6, {}), {2}: (7, {}), {3}: (8, {})} | custom-call | flops 3221225472 | bytes 3670016 | tf_op jit(solution)/shard_map/pallas_call | solution.py:128
  69.9 2.7 %collective-permute-start.14 = (bf16[1024,768]{1,0:T(8,128)(2,1)S(1)}, bf16[1024,768]{1,0:T(8,128)(2,1)S(1)}, u32[]{:S(2)}, u32[]{:S(2)}) collective-permute-start(bf16[1024,768]{1,0:T(8,128)(2,1)S(1)} %get-tuple-element.33.refs_10_), channel_id=1, source_target_pairs={{0,3},{1,0},{2,1},{3,2},{4,7},{5,4},{6,5},{7,6},{8,11},{9,8},{10,9... | collective-permute-start | bytes 4718600 | tf_op jit(solution)/shard_map/ppermute | solution.py:133
  74.8 1.7 collective-permute-start.20
  76.5 6.1 %collective-permute-done.21.refs_6_ = bf16[4,64,768]{2,1,0:T(8,128)(2,1)S(1)} collective-permute-done((bf16[4,64,768]{2,1,0:T(8,128)(2,1)S(1)}, bf16[4,64,768]{2,1,0:T(8,128)(2,1)S(1)}, u32[]{:S(2)}, u32[]{:S(2)}) %collective-permute-start.21) | collective-permute-done | bytes 393248 | tf_op jit(solution)/shard_map/ppermute | solution.py:211
  83.5 22.0 %collective-permute-done.12.refs_11_ = bf16[1024,768]{1,0:T(8,128)(2,1)S(1)} collective-permute-done((bf16[1024,768]{1,0:T(8,128)(2,1)S(1)}, bf16[1024,768]{1,0:T(8,128)(2,1)S(1)}, u32[]{:S(2)}, u32[]{:S(2)}) %collective-permute-start.12) | collective-permute-done | bytes 1572896 | tf_op jit(solution)/shard_map/ppermute | solution.py:133
  107.9 2.7 %collective-permute-start.15 = (bf16[512,768]{1,0:T(8,128)(2,1)}, bf16[512,768]{1,0:T(8,128)(2,1)}, u32[]{:S(2)}, u32[]{:S(2)}) collective-permute-start(bf16[512,768]{1,0:T(8,128)(2,1)} %slice.46), channel_id=1, source_target_pairs={{0,3},{1,0},{2,1},{3,2},{4,7},{5,4},{6,5},{7,6},{8,11},{9,8},{10,9... | collective-permute-start | bytes 2359304 | tf_op jit(solution)/shard_map/ppermute | solution.py:133
  113.5 9.0 %collective-permute-done.3.refs_1_ = bf16[4,128,768]{2,1,0:T(8,128)(2,1)} collective-permute-done((bf16[4,128,768]{2,1,0:T(8,128)(2,1)}, bf16[4,128,768]{2,1,0:T(8,128)(2,1)}, u32[]{:S(2)}, u32[]{:S(2)}) %collective-permute-start.3) | collective-permute-done | bytes 786464 | tf_op jit(solution)/shard_map/ppermute | solution.py:217
  122.8 8.1 %collective-permute-done.23.refs_8_ = bf16[4,64,768]{2,1,0:T(8,128)(2,1)} collective-permute-done((bf16[4,64,768]{2,1,0:T(8,128)(2,1)S(1)}, bf16[4,64,768]{2,1,0:T(8,128)(2,1)}, u32[]{:S(2)}, u32[]{:S(2)}) %collective-permute-start.23) | collective-permute-done | bytes 393248 | tf_op jit(solution)/shard_map/ppermute | solution.py:217
  130.9 1.9 collective-permute-start.5
  132.8 6.6 %collective-permute-done.24.refs_9_ = bf16[4,64,768]{2,1,0:T(8,128)(2,1)} collective-permute-done((bf16[4,64,768]{2,1,0:T(8,128)(2,1)}, bf16[4,64,768]{2,1,0:T(8,128)(2,1)}, u32[]{:S(2)}, u32[]{:S(2)}) %collective-permute-start.24) | collective-permute-done | bytes 393248 | tf_op jit(solution)/shard_map/ppermute | solution.py:217
  139.7 2.4 %collective-permute-start.7 = (bf16[4,128,768]{2,1,0:T(8,128)(2,1)}, bf16[4,128,768]{2,1,0:T(8,128)(2,1)}, u32[]{:S(2)}, u32[]{:S(2)}) collective-permute-start(bf16[4,128,768]{2,1,0:T(8,128)(2,1)} %collective-permute-done.3.refs_1_), channel_id=1, source_target_pairs={{0,12},{4,0},{8,4},{12,8},{16,28},{20,16},{24,20},{28,24},{1,13},{... | collective-permute-start | bytes 2359304 | tf_op jit(solution)/shard_map/ppermute | solution.py:211
  144.4 11.0 %shard_map.97 = bf16[768,768]{1,0:T(8,128)(2,1)} custom-call(s32[10]{0:T(128)S(1)} %stack.56.offs_ref, bf16[4,128,768]{2,1,0:T(8,128)(2,1)S(1)} %copy-done.4, bf16[4,128,768]{2,1,0:T(8,128)(2,1)S(1)} %copy-done.10, bf16[4,128,768]{2,1,0:T(8,128)(2,1)S(1)} %copy-done.6, bf16[4,128,768]{2,1,0:T(8,128)(2,1)S(1)} %copy-done.8, ...), custom_call_target="tpu_custom_call" | custom-call | flops 4831838208 | bytes 13762560 | tf_op jit(solution)/shard_map/pallas_call | solution.py:177
  155.4 8.9 %collective-permute-start.25 = (bf16[768,768]{1,0:T(8,128)(2,1)}, bf16[768,768]{1,0:T(8,128)(2,1)S(1)}, u32[]{:S(2)}, u32[]{:S(2)}) collective-permute-start(bf16[768,768]{1,0:T(8,128)(2,1)} %shard_map.97), channel_id=1, source_target_pairs={{0,224},{32,192},{64,160},{96,128},{128,96},{160,64},{192,32},{224... | collective-permute-start | bytes 3538952 | tf_op jit(solution)/shard_map/ppermute | solution.py:304
  165.5 2.7 %collective-permute-start.9 = (bf16[4,64,768]{2,1,0:T(8,128)(2,1)S(1)}, bf16[4,64,768]{2,1,0:T(8,128)(2,1)S(1)}, u32[]{:S(2)}, u32[]{:S(2)}) collective-permute-start(bf16[4,64,768]{2,1,0:T(8,128)(2,1)S(1)} %slice.42), channel_id=1, source_target_pairs={{0,12},{4,0},{8,4},{12,8},{16,28},{20,16},{24,20},{28,24},{1,13},{... | collective-permute-start | bytes 1179656 | tf_op jit(solution)/shard_map/ppermute | solution.py:211
  170.4 3.0 %collective-permute-start.11 = (bf16[4,64,768]{2,1,0:T(8,128)(2,1)S(1)}, bf16[4,64,768]{2,1,0:T(8,128)(2,1)S(1)}, u32[]{:S(2)}, u32[]{:S(2)}) collective-permute-start(bf16[4,64,768]{2,1,0:T(8,128)(2,1)S(1)} %slice.44), channel_id=1, source_target_pairs={{0,12},{4,0},{8,4},{12,8},{16,28},{20,16},{24,20},{28,24},{1,13},{... | collective-permute-start | bytes 1179656 | tf_op jit(solution)/shard_map/ppermute | solution.py:211
  173.3 3.4 %collective-permute-done.8.refs_6_ = bf16[4,64,768]{2,1,0:T(8,128)(2,1)S(1)} collective-permute-done((bf16[4,64,768]{2,1,0:T(8,128)(2,1)S(1)}, bf16[4,64,768]{2,1,0:T(8,128)(2,1)S(1)}, u32[]{:S(2)}, u32[]{:S(2)}) %collective-permute-start.8) | collective-permute-done | bytes 393248 | tf_op jit(solution)/shard_map/ppermute | solution.py:211
  177.1 5.2 %collective-permute-done.10.refs_8_ = bf16[4,64,768]{2,1,0:T(8,128)(2,1)S(1)} collective-permute-done((bf16[4,64,768]{2,1,0:T(8,128)(2,1)S(1)}, bf16[4,64,768]{2,1,0:T(8,128)(2,1)S(1)}, u32[]{:S(2)}, u32[]{:S(2)}) %collective-permute-start.10) | collective-permute-done | bytes 393248 | tf_op jit(solution)/shard_map/ppermute | solution.py:211
  182.3 2.1 collective-permute-done.11.refs_9_
  184.4 11.3 %shard_map.96 = bf16[768,768]{1,0:T(8,128)(2,1)} custom-call(s32[10]{0:T(128)S(1)} %stack.56.offs_ref, bf16[4,128,768]{2,1,0:T(8,128)(2,1)} %get-tuple-element.40.refs_0_, bf16[4,128,768]{2,1,0:T(8,128)(2,1)} %collective-permute-done.3.refs_1_, bf16[4,128,768]{2,1,0:T(8,128)(2,1)S(1)} %collective-permute-done.4.refs_2_, ...), custom_call_target="tpu_custom_call" | custom-call | flops 4831838208 | bytes 13762560 | tf_op jit(solution)/shard_map/pallas_call | solution.py:177
  195.7 16.8 %collective-permute-done.25 = bf16[768,768]{1,0:T(8,128)(2,1)S(1)} collective-permute-done((bf16[768,768]{1,0:T(8,128)(2,1)}, bf16[768,768]{1,0:T(8,128)(2,1)S(1)}, u32[]{:S(2)}, u32[]{:S(2)}) %collective-permute-start.25) | collective-permute-done | bytes 1179680 | tf_op jit(solution)/shard_map/ppermute | solution.py:304
  212.5 2.6 %fusion = bf16[1,768,768]{2,1,0:T(8,128)(2,1)} fusion(bf16[768,768]{1,0:T(8,128)(2,1)S(1)} %collective-permute-done.25, bf16[768,768]{1,0:T(8,128)(2,1)} %shard_map.96), kind=kLoop, calls=%fused_computation.3 | loop fusion | flops 2359296 | bytes 3538944 | tf_op jit(solution)/shard_map/broadcast_in_dim | solution.py:308
  (79 shorter events, 20.1 us)
Async XLA Ops:
  7.4 18.8 %collective-permute-start.2 = (bf16[2,128,768]{2,1,0:T(8,128)(2,1)}, bf16[2,128,768]{2,1,0:T(8,128)(2,1)}, u32[]{:S(2)}, u32[]{:S(2)}) collective-permute-start(bf16[2,128,768]{2,1,0:T(8,128)(2,1)} %get-tuple-element.43), channel_id=1, source_target_pairs={{0,3},{1,0},{2,1},{3,2},{4,7},{5,4},{6,5},{7,6},{8,11},{9,8},{10,9... | collective-permute-start | bytes 1179656 | tf_op jit(solution)/shard_map/ppermute | solution.py:133
  10.7 15.6 %collective-permute-start.1 = (bf16[2,128,768]{2,1,0:T(8,128)(2,1)}, bf16[2,128,768]{2,1,0:T(8,128)(2,1)}, u32[]{:S(2)}, u32[]{:S(2)}) collective-permute-start(bf16[2,128,768]{2,1,0:T(8,128)(2,1)} %get-tuple-element.44), channel_id=1, source_target_pairs={{0,2},{1,3},{2,0},{3,1},{4,6},{5,7},{6,4},{7,5},{8,10},{9,11},{10,... | collective-permute-start | bytes 1179656 | tf_op jit(solution)/shard_map/ppermute | solution.py:133
  11.2 20.8 %collective-permute-start = (bf16[2,128,768]{2,1,0:T(8,128)(2,1)}, bf16[2,128,768]{2,1,0:T(8,128)(2,1)}, u32[]{:S(2)}, u32[]{:S(2)}) collective-permute-start(bf16[2,128,768]{2,1,0:T(8,128)(2,1)} %get-tuple-element.45), channel_id=1, source_target_pairs={{0,1},{1,2},{2,3},{3,0},{4,5},{5,6},{6,7},{7,4},{8,9},{9,10},{10,1... | collective-permute-start | bytes 1179656 | tf_op jit(solution)/shard_map/ppermute | solution.py:133
  34.4 19.0 %collective-permute-start.16 = (bf16[4,128,768]{2,1,0:T(8,128)(2,1)S(1)}, bf16[4,128,768]{2,1,0:T(8,128)(2,1)S(1)}, u32[]{:S(2)}, u32[]{:S(2)}) collective-permute-start(bf16[4,128,768]{2,1,0:T(8,128)(2,1)S(1)} %get-tuple-element.34.refs_0_), channel_id=1, source_target_pairs={{0,16},{4,20},{8,24},{12,28},{16,0},{20,4},{24,8},{28,12},{1,17},{... | collective-permute-start | bytes 2359304 | tf_op jit(solution)/shard_map/ppermute | solution.py:217
  36.1 19.7 %collective-permute-start.17 = (bf16[4,128,768]{2,1,0:T(8,128)(2,1)S(1)}, bf16[4,128,768]{2,1,0:T(8,128)(2,1)S(1)}, u32[]{:S(2)}, u32[]{:S(2)}) collective-permute-start(bf16[4,128,768]{2,1,0:T(8,128)(2,1)S(1)} %get-tuple-element.34.refs_0_), channel_id=1, source_target_pairs={{0,4},{4,8},{8,12},{12,0},{16,20},{20,24},{24,28},{28,16},{1,5},{5... | collective-permute-start | bytes 2359304 | tf_op jit(solution)/shard_map/ppermute | solution.py:211
  37.4 18.4 %collective-permute-start.18 = (bf16[4,128,768]{2,1,0:T(8,128)(2,1)S(1)}, bf16[4,128,768]{2,1,0:T(8,128)(2,1)S(1)}, u32[]{:S(2)}, u32[]{:S(2)}) collective-permute-start(bf16[4,128,768]{2,1,0:T(8,128)(2,1)S(1)} %get-tuple-element.34.refs_0_), channel_id=1, source_target_pairs={{0,12},{4,0},{8,4},{12,8},{16,28},{20,16},{24,20},{28,24},{1,13},{... | collective-permute-start | bytes 2359304 | tf_op jit(solution)/shard_map/ppermute | solution.py:211
  53.4 21.4 %copy-start.9 = (bf16[4,128,768]{2,1,0:T(8,128)(2,1)}, bf16[4,128,768]{2,1,0:T(8,128)(2,1)S(1)}, u32[]{:S(2)}) copy-start(bf16[4,128,768]{2,1,0:T(8,128)(2,1)S(1)} %collective-permute-done.16.refs_1_) | copy-start | bytes 2359300
  55.7 20.7 %copy-start.7 = (bf16[4,128,768]{2,1,0:T(8,128)(2,1)}, bf16[4,128,768]{2,1,0:T(8,128)(2,1)S(1)}, u32[]{:S(2)}) copy-start(bf16[4,128,768]{2,1,0:T(8,128)(2,1)S(1)} %collective-permute-done.18.refs_3_) | copy-start | bytes 2359300
  69.9 37.0 %copy-start.2 = (bf16[1024,768]{1,0:T(8,128)(2,1)}, bf16[1024,768]{1,0:T(8,128)(2,1)S(1)}, u32[]{:S(2)}) copy-start(bf16[1024,768]{1,0:T(8,128)(2,1)S(1)} %get-tuple-element.33.refs_10_) | copy-start | bytes 4718596
  69.9 35.6 %collective-permute-start.12 = (bf16[1024,768]{1,0:T(8,128)(2,1)S(1)}, bf16[1024,768]{1,0:T(8,128)(2,1)S(1)}, u32[]{:S(2)}, u32[]{:S(2)}) collective-permute-start(bf16[1024,768]{1,0:T(8,128)(2,1)S(1)} %get-tuple-element.33.refs_10_), channel_id=1, source_target_pairs={{0,1},{1,2},{2,3},{3,0},{4,5},{5,6},{6,7},{7,4},{8,9},{9,10},{10,1... | collective-permute-start | bytes 4718600 | tf_op jit(solution)/shard_map/ppermute | solution.py:133
  69.9 37.0 %collective-permute-start.14 = (bf16[1024,768]{1,0:T(8,128)(2,1)S(1)}, bf16[1024,768]{1,0:T(8,128)(2,1)S(1)}, u32[]{:S(2)}, u32[]{:S(2)}) collective-permute-start(bf16[1024,768]{1,0:T(8,128)(2,1)S(1)} %get-tuple-element.33.refs_10_), channel_id=1, source_target_pairs={{0,3},{1,0},{2,1},{3,2},{4,7},{5,4},{6,5},{7,6},{8,11},{9,8},{10,9... | collective-permute-start | bytes 4718600 | tf_op jit(solution)/shard_map/ppermute | solution.py:133
  72.6 10.0 %collective-permute-start.21 = (bf16[4,64,768]{2,1,0:T(8,128)(2,1)S(1)}, bf16[4,64,768]{2,1,0:T(8,128)(2,1)S(1)}, u32[]{:S(2)}, u32[]{:S(2)}) collective-permute-start(bf16[4,64,768]{2,1,0:T(8,128)(2,1)S(1)} %slice.38), channel_id=1, source_target_pairs={{0,4},{4,8},{8,12},{12,0},{16,20},{20,24},{24,28},{28,16},{1,5},{5... | collective-permute-start | bytes 1179656 | tf_op jit(solution)/shard_map/ppermute | solution.py:211
  73.8 36.8 %collective-permute-start.19 = (bf16[4,128,768]{2,1,0:T(8,128)(2,1)S(1)}, bf16[4,128,768]{2,1,0:T(8,128)(2,1)S(1)}, u32[]{:S(2)}, u32[]{:S(2)}) collective-permute-start(bf16[4,128,768]{2,1,0:T(8,128)(2,1)S(1)} %collective-permute-done.16.refs_1_), channel_id=1, source_target_pairs={{0,4},{4,8},{8,12},{12,0},{16,20},{20,24},{24,28},{28,16},{1,5},{5... | collective-permute-start | bytes 2359304 | tf_op jit(solution)/shard_map/ppermute | solution.py:211
  74.8 36.7 %collective-permute-start.20 = (bf16[4,128,768]{2,1,0:T(8,128)(2,1)S(1)}, bf16[4,128,768]{2,1,0:T(8,128)(2,1)S(1)}, u32[]{:S(2)}, u32[]{:S(2)}) collective-permute-start(bf16[4,128,768]{2,1,0:T(8,128)(2,1)S(1)} %collective-permute-done.16.refs_1_), channel_id=1, source_target_pairs={{0,12},{4,0},{8,4},{12,8},{16,28},{20,16},{24,20},{28,24},{1,13},{... | collective-permute-start | bytes 2359304 | tf_op jit(solution)/shard_map/ppermute | solution.py:211
  82.6 25.3 %collective-permute-start.22 = (bf16[4,64,768]{2,1,0:T(8,128)(2,1)S(1)}, bf16[4,64,768]{2,1,0:T(8,128)(2,1)}, u32[]{:S(2)}, u32[]{:S(2)}) collective-permute-start(bf16[4,64,768]{2,1,0:T(8,128)(2,1)S(1)} %slice.39), channel_id=1, source_target_pairs={{0,12},{4,0},{8,4},{12,8},{16,28},{20,16},{24,20},{28,24},{1,13},{... | collective-permute-start | bytes 1179656 | tf_op jit(solution)/shard_map/ppermute | solution.py:211
  105.4 36.7 %copy-start.4 = (bf16[4,128,768]{2,1,0:T(8,128)(2,1)S(1)}, bf16[4,128,768]{2,1,0:T(8,128)(2,1)}, u32[]{:S(2)}) copy-start(bf16[4,128,768]{2,1,0:T(8,128)(2,1)} %copy-done.3) | copy-start | bytes 2359300
  105.4 36.7 %copy-start.6 = (bf16[4,128,768]{2,1,0:T(8,128)(2,1)S(1)}, bf16[4,128,768]{2,1,0:T(8,128)(2,1)}, u32[]{:S(2)}) copy-start(bf16[4,128,768]{2,1,0:T(8,128)(2,1)} %copy-done.5) | copy-start | bytes 2359300
  105.4 36.7 %copy-start.8 = (bf16[4,128,768]{2,1,0:T(8,128)(2,1)S(1)}, bf16[4,128,768]{2,1,0:T(8,128)(2,1)}, u32[]{:S(2)}) copy-start(bf16[4,128,768]{2,1,0:T(8,128)(2,1)} %copy-done.7) | copy-start | bytes 2359300
  105.4 17.1 %collective-permute-start.3 = (bf16[4,128,768]{2,1,0:T(8,128)(2,1)}, bf16[4,128,768]{2,1,0:T(8,128)(2,1)}, u32[]{:S(2)}, u32[]{:S(2)}) collective-permute-start(bf16[4,128,768]{2,1,0:T(8,128)(2,1)} %get-tuple-element.40.refs_0_), channel_id=1, source_target_pairs={{0,16},{4,20},{8,24},{12,28},{16,0},{20,4},{24,8},{28,12},{1,17},{... | collective-permute-start | bytes 2359304 | tf_op jit(solution)/shard_map/ppermute | solution.py:217
  106.9 32.8 %collective-permute-start.13 = (bf16[512,768]{1,0:T(8,128)(2,1)}, bf16[512,768]{1,0:T(8,128)(2,1)}, u32[]{:S(2)}, u32[]{:S(2)}) collective-permute-start(bf16[512,768]{1,0:T(8,128)(2,1)} %slice.45), channel_id=1, source_target_pairs={{0,1},{1,2},{2,3},{3,0},{4,5},{5,6},{6,7},{7,4},{8,9},{9,10},{10,1... | collective-permute-start | bytes 2359304 | tf_op jit(solution)/shard_map/ppermute | solution.py:133
  107.9 34.2 %collective-permute-start.15 = (bf16[512,768]{1,0:T(8,128)(2,1)}, bf16[512,768]{1,0:T(8,128)(2,1)}, u32[]{:S(2)}, u32[]{:S(2)}) collective-permute-start(bf16[512,768]{1,0:T(8,128)(2,1)} %slice.46), channel_id=1, source_target_pairs={{0,3},{1,0},{2,1},{3,2},{4,7},{5,4},{6,5},{7,6},{8,11},{9,8},{10,9... | collective-permute-start | bytes 2359304 | tf_op jit(solution)/shard_map/ppermute | solution.py:133
  111.5 19.5 %collective-permute-start.23 = (bf16[4,64,768]{2,1,0:T(8,128)(2,1)S(1)}, bf16[4,64,768]{2,1,0:T(8,128)(2,1)}, u32[]{:S(2)}, u32[]{:S(2)}) collective-permute-start(bf16[4,64,768]{2,1,0:T(8,128)(2,1)S(1)} %collective-permute-done.21.refs_6_), channel_id=1, source_target_pairs={{0,16},{4,20},{8,24},{12,28},{16,0},{20,4},{24,8},{28,12},{1,17},{... | collective-permute-start | bytes 1179656 | tf_op jit(solution)/shard_map/ppermute | solution.py:217
  112.7 26.7 %collective-permute-start.24 = (bf16[4,64,768]{2,1,0:T(8,128)(2,1)}, bf16[4,64,768]{2,1,0:T(8,128)(2,1)}, u32[]{:S(2)}, u32[]{:S(2)}) collective-permute-start(bf16[4,64,768]{2,1,0:T(8,128)(2,1)} %collective-permute-done.22.refs_7_), channel_id=1, source_target_pairs={{0,16},{4,20},{8,24},{12,28},{16,0},{20,4},{24,8},{28,12},{1,17},{... | collective-permute-start | bytes 1179656 | tf_op jit(solution)/shard_map/ppermute | solution.py:217
  122.5 41.8 %collective-permute-start.4 = (bf16[4,128,768]{2,1,0:T(8,128)(2,1)}, bf16[4,128,768]{2,1,0:T(8,128)(2,1)S(1)}, u32[]{:S(2)}, u32[]{:S(2)}) collective-permute-start(bf16[4,128,768]{2,1,0:T(8,128)(2,1)} %get-tuple-element.40.refs_0_), channel_id=1, source_target_pairs={{0,4},{4,8},{8,12},{12,0},{16,20},{20,24},{24,28},{28,16},{1,5},{5... | collective-permute-start | bytes 2359304 | tf_op jit(solution)/shard_map/ppermute | solution.py:211
  130.9 33.5 %collective-permute-start.5 = (bf16[4,128,768]{2,1,0:T(8,128)(2,1)}, bf16[4,128,768]{2,1,0:T(8,128)(2,1)}, u32[]{:S(2)}, u32[]{:S(2)}) collective-permute-start(bf16[4,128,768]{2,1,0:T(8,128)(2,1)} %get-tuple-element.40.refs_0_), channel_id=1, source_target_pairs={{0,12},{4,0},{8,4},{12,8},{16,28},{20,16},{24,20},{28,24},{1,13},{... | collective-permute-start | bytes 2359304 | tf_op jit(solution)/shard_map/ppermute | solution.py:211
  139.4 28.8 %collective-permute-start.6 = (bf16[4,128,768]{2,1,0:T(8,128)(2,1)}, bf16[4,128,768]{2,1,0:T(8,128)(2,1)}, u32[]{:S(2)}, u32[]{:S(2)}) collective-permute-start(bf16[4,128,768]{2,1,0:T(8,128)(2,1)} %collective-permute-done.3.refs_1_), channel_id=1, source_target_pairs={{0,4},{4,8},{8,12},{12,0},{16,20},{20,24},{24,28},{28,16},{1,5},{5... | collective-permute-start | bytes 2359304 | tf_op jit(solution)/shard_map/ppermute | solution.py:211
  139.7 29.6 %collective-permute-start.7 = (bf16[4,128,768]{2,1,0:T(8,128)(2,1)}, bf16[4,128,768]{2,1,0:T(8,128)(2,1)}, u32[]{:S(2)}, u32[]{:S(2)}) collective-permute-start(bf16[4,128,768]{2,1,0:T(8,128)(2,1)} %collective-permute-done.3.refs_1_), channel_id=1, source_target_pairs={{0,12},{4,0},{8,4},{12,8},{16,28},{20,16},{24,20},{28,24},{1,13},{... | collective-permute-start | bytes 2359304 | tf_op jit(solution)/shard_map/ppermute | solution.py:211
  155.4 57.1 %collective-permute-start.25 = (bf16[768,768]{1,0:T(8,128)(2,1)}, bf16[768,768]{1,0:T(8,128)(2,1)S(1)}, u32[]{:S(2)}, u32[]{:S(2)}) collective-permute-start(bf16[768,768]{1,0:T(8,128)(2,1)} %shard_map.97), channel_id=1, source_target_pairs={{0,224},{32,192},{64,160},{96,128},{128,96},{160,64},{192,32},{224... | collective-permute-start | bytes 3538952 | tf_op jit(solution)/shard_map/ppermute | solution.py:304
  164.3 12.4 %collective-permute-start.8 = (bf16[4,64,768]{2,1,0:T(8,128)(2,1)S(1)}, bf16[4,64,768]{2,1,0:T(8,128)(2,1)S(1)}, u32[]{:S(2)}, u32[]{:S(2)}) collective-permute-start(bf16[4,64,768]{2,1,0:T(8,128)(2,1)S(1)} %slice.41), channel_id=1, source_target_pairs={{0,4},{4,8},{8,12},{12,0},{16,20},{20,24},{24,28},{28,16},{1,5},{5... | collective-permute-start | bytes 1179656 | tf_op jit(solution)/shard_map/ppermute | solution.py:211
  165.5 11.7 %collective-permute-start.9 = (bf16[4,64,768]{2,1,0:T(8,128)(2,1)S(1)}, bf16[4,64,768]{2,1,0:T(8,128)(2,1)S(1)}, u32[]{:S(2)}, u32[]{:S(2)}) collective-permute-start(bf16[4,64,768]{2,1,0:T(8,128)(2,1)S(1)} %slice.42), channel_id=1, source_target_pairs={{0,12},{4,0},{8,4},{12,8},{16,28},{20,16},{24,20},{28,24},{1,13},{... | collective-permute-start | bytes 1179656 | tf_op jit(solution)/shard_map/ppermute | solution.py:211
  169.2 13.1 %collective-permute-start.10 = (bf16[4,64,768]{2,1,0:T(8,128)(2,1)S(1)}, bf16[4,64,768]{2,1,0:T(8,128)(2,1)S(1)}, u32[]{:S(2)}, u32[]{:S(2)}) collective-permute-start(bf16[4,64,768]{2,1,0:T(8,128)(2,1)S(1)} %slice.43), channel_id=1, source_target_pairs={{0,4},{4,8},{8,12},{12,0},{16,20},{20,24},{24,28},{28,16},{1,5},{5... | collective-permute-start | bytes 1179656 | tf_op jit(solution)/shard_map/ppermute | solution.py:211
  170.4 14.1 %collective-permute-start.11 = (bf16[4,64,768]{2,1,0:T(8,128)(2,1)S(1)}, bf16[4,64,768]{2,1,0:T(8,128)(2,1)S(1)}, u32[]{:S(2)}, u32[]{:S(2)}) collective-permute-start(bf16[4,64,768]{2,1,0:T(8,128)(2,1)S(1)} %slice.44), channel_id=1, source_target_pairs={{0,12},{4,0},{8,4},{12,8},{16,28},{20,16},{24,20},{28,24},{1,13},{... | collective-permute-start | bytes 1179656 | tf_op jit(solution)/shard_map/ppermute | solution.py:211
  (12 other events, 89.9 us)
